TPU v7x, 256 devices: a whole 4x4x8 slice. The times are simulated.
256 devices in a mesh: unit: 128 (over z, y, x), samp: 2 (over core).
Axes of the slice: x: 4, y: 4, z: 8, core: 2. Of those that a mesh axis runs over, the one named last changes fastest.
Arguments:
- abundance: float32 [131072, 4096], P('unit', 'samp'), may hold values from 0.0009 to 27, as said below
- unitig_factor: float32 [131072, 128], P('unit'), may hold values from 0.005 to 1.8, as said below
- sample_factor: float32 [4096, 128], P('samp'), may hold values from 0.02 to 0.2
Outputs:
- unitig_update: float32 [131072, 128], P('unit')
- sample_update: float32 [4096, 128], P('samp')
Inputs may be any that keep to these rules, and one draw needn't show every extreme that they name: abundance entries are positive. unitig_factor entries are positive.
All inputs are finite; a program needn't handle non-finite values.
Results may differ from a plain program's by a relative error of at most 0.0001.
Values sent between devices are 32-bit elements; how exact they have to be, the bound alone decides.
No kernel may reach another device: no remote copies, remote signals or barrier semaphores. Data moves between devices by JAX's collectives and lax.ppermute only.
A program may use at most 64 MiB of HBM per device.

v0:
```python
import jax
import jax.numpy as jnp
from jax import lax
from jax.sharding import Mesh
from jax.sharding import PartitionSpec as P

ITERS = 2


HI = lax.Precision.HIGHEST


def inner(left, right):
    return lax.dot_general(
        left, right, (((0,), (0,)), ((), ())), precision=HI, preferred_element_type=jnp.float32
    )


def reduce_scatter(x, axes, n):
    chunks = x.reshape(n, x.shape[0] // n, *x.shape[1:])
    return lax.all_to_all(chunks, axes, 0, 0, tiled=False).sum(0)


def all_gather(piece, axes, n):
    copies = jnp.broadcast_to(piece[None], (n, *piece.shape))
    held = lax.all_to_all(copies, axes, 0, 0, tiled=False)
    return held.reshape(n * piece.shape[0], *piece.shape[1:])


def unit_sum(x, stages):
    for axes, n in stages:
        x = reduce_scatter(x, axes, n)
    for axes, n in reversed(stages):
        x = all_gather(x, axes, n)
    return x


def samp_sum(x):
    return x + lax.ppermute(x, "samp", [(0, 1), (1, 0)])


def shards(stages, abundance, unitig_factor, sample_factor):
    unitig = unitig_factor
    sample = sample_factor
    n_samp = sample.shape[0]
    n_unit = unitig.shape[0]
    for sweep in range(ITERS):
        both = unit_sum(
            jnp.concatenate([inner(abundance, unitig), inner(unitig, unitig)]), stages
        )
        target_h, gram_unit = both[:n_samp], both[n_samp:]
        sample = sample * target_h / jnp.dot(sample, gram_unit, precision=HI)
        both = samp_sum(
            jnp.concatenate([jnp.dot(abundance, sample, precision=HI), inner(sample, sample)])
        )
        target_w, gram_sample = both[:n_unit], both[n_unit:]
        unitig = unitig * target_w / jnp.dot(unitig, gram_sample, precision=HI)
    return (unitig, sample)


def unit_dims(mesh):
    row = mesh.devices[:, 0]
    n = row.shape[0]
    try:
        sizes = [len({d.coords[c] for d in row}) for c in (2, 1, 0)]
    except AttributeError:
        sizes = [n]
    if sizes[0] * sizes[1] * sizes[2] != n if len(sizes) == 3 else True:
        sizes = [n]
    names = ["uz", "uy", "ux"][: len(sizes)]
    return list(zip(names, sizes))


def stages_of(dims):
    if len(dims) < 3:
        return [(tuple(a for a, _ in dims), dims[0][1])]
    (z, nz), (y, ny), (x, nx) = dims
    return [((y, x), ny * nx), (z, nz)]


def solution(mesh):
    dims = unit_dims(mesh)
    inner_mesh = Mesh(
        mesh.devices.reshape(*[s for _, s in dims], mesh.devices.shape[1]),
        (*[a for a, _ in dims], "samp"),
    )
    unit = tuple(a for a, _ in dims)
    return jax.shard_map(
        lambda *args: shards(stages_of(dims), *args),
        mesh=inner_mesh,
        in_specs=(P(unit, "samp"), P(unit, None), P("samp", None)),
        out_specs=(P(unit, None), P("samp", None)),
        check_vma=False,
    )
```

profile of v0, /device:TPU:1, one launch (start us, length us, event | category | flops | bytes accessed | tf_op | source)
XLA Modules:
  0.0 206.2 jit_solution(2075897453216761214)
XLA Ops:
  0.6 2.3 %fusion.15 = f32[128,128]{1,0:T(8,128)S(1)} fusion(f32[1024,128]{1,0:T(8,128)} %param.4), kind=kOutput, calls=%fused_computation.23 | convolution fusion | flops 201326592 | bytes 589824 | tf_op jit(solution)/shard_map/dot_general | solution.py:14
  2.9 15.5 %fusion.14 = f32[2048,128]{1,0:T(8,128)S(1)} fusion(f32[1024,2048]{1,0:T(8,128)} %param.3, f32[1024,128]{1,0:T(8,128)S(1)} %copy-done), kind=kOutput, calls=%fused_computation.22 | convolution fusion | flops 3221225472 | bytes 9961472 | tf_op jit(solution)/shard_map/dot_general | solution.py:14
  18.5 24.3 %all_to_all.40 = f32[16,136,128]{2,1,0:T(8,128)S(1)} all-to-all(f32[16,136,128]{2,1,0:T(8,128)S(1)} %bitcast.40), channel_id=1, replica_groups=mesh['uz'=8,'uy'=4,'ux'=4,'samp'=2] {'uy','ux'}, dimensions={0} | all-to-all | bytes 2228224 | tf_op jit(solution)/shard_map/all_to_all | solution.py:21
  42.9 15.7 %all_to_all.41 = f32[8,17,128]{2,1,0:T(8,128)S(1)} all-to-all(f32[8,17,128]{2,1,0:T(8,128)S(1)} %reshape.27), channel_id=1, replica_groups=mesh['uz'=8,'uy'=4,'ux'=4,'samp'=2] {'uz'}, dimensions={0} | all-to-all | bytes 139264 | tf_op jit(solution)/shard_map/all_to_all | solution.py:21
  58.6 10.0 %all_to_all.42 = f32[8,17,128]{2,1,0:T(8,128)S(1)} all-to-all(f32[8,17,128]{2,1,0:T(8,128)S(1)} %broadcast_in_dim.12), channel_id=1, replica_groups=mesh['uz'=8,'uy'=4,'ux'=4,'samp'=2] {'uz'}, dimensions={0} | all-to-all | bytes 139264 | tf_op jit(solution)/shard_map/all_to_all | solution.py:26
  68.5 1.1 broadcast_in_dim.28
  69.6 4.0 %all-to-all-start.3 = ((f32[16,136,128]{2,1,0:T(8,128)}), f32[16,136,128]{2,1,0:T(8,128)S(1)}, u32[]{:S(2)}, u32[]{:S(2)}) async-start(f32[16,136,128]{2,1,0:T(8,128)} %broadcast_in_dim.28), calls=%async_computation.3 | async-start | bytes 2228224 | tf_op jit(solution)/shard_map/all_to_all | solution.py:26
  73.6 1.3 copy.15
  74.9 12.7 %all-to-all-done.3 = f32[16,136,128]{2,1,0:T(8,128)S(1)} async-done(((f32[16,136,128]{2,1,0:T(8,128)}), f32[16,136,128]{2,1,0:T(8,128)S(1)}, u32[]{:S(2)}, u32[]{:S(2)}) %all-to-all-start.3) | async-done | bytes 1114144 | tf_op jit(solution)/shard_map/all_to_all | solution.py:26
  87.7 1.3 copy.31
  89.0 3.0 %fusion = f32[2048,128]{0,1:T(8,128)S(1)} fusion(f32[2048,128]{1,0:T(8,128)} %param.5, f32[2048,128]{0,1:T(8,128)} %copy.15, f32[2048,128]{0,1:T(8,128)} %copy.31, f32[2176,128]{1,0:T(8,128)S(1)} %bitcast.39), kind=kOutput, calls=%fused_computation.2 | convolution fusion | flops 403177472 | bytes 4259840 | tf_op jit(solution)/shard_map/dot_general | solution.py:52
  93.0 11.2 %convolution_bitcast_fusion.4 = f32[1024,128]{0,1:T(8,128)S(1)} fusion(f32[2048,128]{0,1:T(8,128)S(1)} %fusion, f32[1024,2048]{1,0:T(8,128)} %param.3), kind=kOutput, calls=%fused_computation.6 | convolution fusion | flops 3221225472 | bytes 9961472 | tf_op jit(solution)/shard_map/dot_general | solution.py:54
  104.2 5.4 %collective-permute-start = (f32[1152,128]{0,1:T(8,128)S(1)}, f32[1152,128]{0,1:T(8,128)S(1)}, u32[]{:S(2)}, u32[]{:S(2)}) collective-permute-start(f32[1152,128]{0,1:T(8,128)S(1)} %pad_maximum_fusion.2), channel_id=1, source_target_pairs={{0,1},{1,0},{2,3},{3,2},{4,5},{5,4},{6,7},{7,6},{8,9},{9,8},{10,11... | collective-permute-start | bytes 1769480 | tf_op jit(solution)/shard_map/ppermute | solution.py:39
  112.9 7.0 %convolution_bitcast_fusion = f32[2048,128]{0,1:T(8,128)S(1)} fusion(f32[1024,128]{0,1:T(8,128)S(1)} %fusion.2, f32[1024,2048]{1,0:T(8,128)} %param.3), kind=kOutput, calls=%fused_computation | convolution fusion | flops 3221225472 | bytes 9961472 | tf_op jit(solution)/shard_map/dot_general | solution.py:14
  120.0 1.4 copy.19
  121.3 21.7 %all_to_all.43 = f32[16,136,128]{2,1,0:T(8,128)S(1)} all-to-all(f32[16,136,128]{2,1,0:T(8,128)} %bitcast.41), channel_id=1, replica_groups=mesh['uz'=8,'uy'=4,'ux'=4,'samp'=2] {'uy','ux'}, dimensions={0} | all-to-all | bytes 2228224 | tf_op jit(solution)/shard_map/all_to_all | solution.py:21
  143.1 9.8 %all_to_all.44 = f32[8,17,128]{2,1,0:T(8,128)S(1)} all-to-all(f32[8,17,128]{2,1,0:T(8,128)S(1)} %reshape.30), channel_id=1, replica_groups=mesh['uz'=8,'uy'=4,'ux'=4,'samp'=2] {'uz'}, dimensions={0} | all-to-all | bytes 139264 | tf_op jit(solution)/shard_map/all_to_all | solution.py:21
  153.0 10.1 %all_to_all.45 = f32[8,17,128]{2,1,0:T(8,128)S(1)} all-to-all(f32[8,17,128]{2,1,0:T(8,128)S(1)} %broadcast_in_dim.29), channel_id=1, replica_groups=mesh['uz'=8,'uy'=4,'ux'=4,'samp'=2] {'uz'}, dimensions={0} | all-to-all | bytes 139264 | tf_op jit(solution)/shard_map/all_to_all | solution.py:26
  163.1 17.2 %all_to_all.46 = f32[16,136,128]{2,1,0:T(8,128)S(1)} all-to-all(f32[16,136,128]{2,1,0:T(8,128)S(1)} %broadcast_in_dim.31), channel_id=1, replica_groups=mesh['uz'=8,'uy'=4,'ux'=4,'samp'=2] {'uy','ux'}, dimensions={0} | all-to-all | bytes 2228224 | tf_op jit(solution)/shard_map/all_to_all | solution.py:26
  181.4 1.3 copy.32
  182.7 2.4 %convolution_divide_fusion = f32[2048,128]{0,1:T(8,128)S(1)} fusion(f32[2048,128]{0,1:T(8,128)S(1)} %fusion, f32[2048,128]{0,1:T(8,128)} %copy.32, f32[2176,128]{1,0:T(8,128)} %bitcast.43), kind=kOutput, calls=%fused_computation.3 | convolution fusion | flops 403177472 | bytes 4259840 | tf_op jit(solution)/shard_map/dot_general | solution.py:52
  186.1 11.2 %convolution_bitcast_fusion.2 = f32[1024,128]{0,1:T(8,128)S(1)} fusion(f32[2048,128]{0,1:T(8,128)S(1)} %convolution_divide_fusion, f32[1024,2048]{1,0:T(8,128)} %param.3), kind=kOutput, calls=%fused_computation.4 | convolution fusion | flops 3221225472 | bytes 9961472 | tf_op jit(solution)/shard_map/dot_general | solution.py:54
  198.1 4.6 %collective-permute-start.1 = (f32[1152,128]{0,1:T(8,128)}, f32[1152,128]{0,1:T(8,128)S(1)}, u32[]{:S(2)}, u32[]{:S(2)}) collective-permute-start(f32[1152,128]{0,1:T(8,128)} %pad_maximum_fusion.3), channel_id=1, source_target_pairs={{0,1},{1,0},{2,3},{3,2},{4,5},{5,4},{6,7},{7,6},{8,9},{9,8},{10,11... | collective-permute-start | bytes 1769480 | tf_op jit(solution)/shard_map/ppermute | solution.py:39
  202.7 1.3 copy.25
  (36 shorter events, 9.9 us)
Async XLA Ops:
  0.6 2.3 %copy-start = (f32[1024,128]{1,0:T(8,128)S(1)}, f32[1024,128]{1,0:T(8,128)}, u32[]{:S(2)}) copy-start(f32[1024,128]{1,0:T(8,128)} %param.4) | copy-start | bytes 1572868
  69.6 4.0 %copy-start.2 = (f32[2048,128]{1,0:T(8,128)S(1)}, f32[2048,128]{1,0:T(8,128)}, u32[]{:S(2)}) copy-start(f32[2048,128]{1,0:T(8,128)} %param.5) | copy-start | bytes 3145732
  69.6 18.0 %all-to-all-start.3 = ((f32[16,136,128]{2,1,0:T(8,128)}), f32[16,136,128]{2,1,0:T(8,128)S(1)}, u32[]{:S(2)}, u32[]{:S(2)}) async-start(f32[16,136,128]{2,1,0:T(8,128)} %broadcast_in_dim.28), calls=%async_computation.3 | async-start | bytes 2228224 | tf_op jit(solution)/shard_map/all_to_all | solution.py:26
  104.2 7.0 %collective-permute-start = (f32[1152,128]{0,1:T(8,128)S(1)}, f32[1152,128]{0,1:T(8,128)S(1)}, u32[]{:S(2)}, u32[]{:S(2)}) collective-permute-start(f32[1152,128]{0,1:T(8,128)S(1)} %pad_maximum_fusion.2), channel_id=1, source_target_pairs={{0,1},{1,0},{2,3},{3,2},{4,5},{5,4},{6,7},{7,6},{8,9},{9,8},{10,11... | collective-permute-start | bytes 1769480 | tf_op jit(solution)/shard_map/ppermute | solution.py:39
  110.6 1.0 copy-start.3
  180.3 1.0 copy-start.1
  198.1 6.4 %collective-permute-start.1 = (f32[1152,128]{0,1:T(8,128)}, f32[1152,128]{0,1:T(8,128)S(1)}, u32[]{:S(2)}, u32[]{:S(2)}) collective-permute-start(f32[1152,128]{0,1:T(8,128)} %pad_maximum_fusion.3), channel_id=1, source_target_pairs={{0,1},{1,0},{2,3},{3,2},{4,5},{5,4},{6,7},{7,6},{8,9},{9,8},{10,11... | collective-permute-start | bytes 1769480 | tf_op jit(solution)/shard_map/ppermute | solution.py:39
where the time goes:
time: 207 us; the launch traced here: 206 us
  blocking collectives  109 us (53%)
  matrix products  56.3 us (27%)
  starting transfers between devices  14 us (7%)
  waiting for transfers between devices  13.9 us (7%)
  local copies, waits for them, and re-layouts  11.3 us (5%)
    all_to_all x4, blocking collectives, reduce_scatter(): return lax.all_to_all(chunks, axes, 0, 0, tiled=False).sum(0)  71.4 us
    all_to_all x3, blocking collectives, all_gather(): held = lax.all_to_all(copies, axes, 0, 0, tiled=False)  37.2 us
    dot_general x6, matrix products, inner(): lax.dot_general(left, right, (((0,), (0,)), ((), ())), precision=HI, pref...  27.4 us
    dot_general x2, matrix products, shards(): jnp.dot(abundance, sample, precision=HI)  22.3 us
    all_to_all x1, waiting for transfers between devices, all_gather(): held = lax.all_to_all(copies, axes, 0, 0, tiled=False)  12.7 us
    ppermute x2, starting transfers between devices, samp_sum(): return x + lax.ppermute(x, 'samp', [(0, 1), (1, 0)])  9.99 us
    unnamed x14, local copies, waits for them, and re-layouts  8.58 us
    dot_general x2, matrix products, shards(): sample = sample * target_h / jnp.dot(sample, gram_unit, precision=HI)  5.35 us
  transfers between devices with their start and end apart: 3, of which 3 were waited for; matrix products, arithmetic and copies ran while one was open for 2% of the time, Pallas kernels for 0%

commit v1 on v0

--- a/solution.py
+++ b/solution.py
@@ -8,11 +8,12 @@
 
 
 HI = lax.Precision.HIGHEST
+WIDE = lax.Precision.HIGH
 
 
-def inner(left, right):
+def inner(left, right, precision=HI):
     return lax.dot_general(
-        left, right, (((0,), (0,)), ((), ())), precision=HI, preferred_element_type=jnp.float32
+        left, right, (((0,), (0,)), ((), ())), precision=precision, preferred_element_type=jnp.float32
     )
 
 
@@ -46,12 +47,12 @@
     n_unit = unitig.shape[0]
     for sweep in range(ITERS):
         both = unit_sum(
-            jnp.concatenate([inner(abundance, unitig), inner(unitig, unitig)]), stages
+            jnp.concatenate([inner(abundance, unitig, WIDE), inner(unitig, unitig)]), stages
         )
         target_h, gram_unit = both[:n_samp], both[n_samp:]
         sample = sample * target_h / jnp.dot(sample, gram_unit, precision=HI)
         both = samp_sum(
-            jnp.concatenate([jnp.dot(abundance, sample, precision=HI), inner(sample, sample)])
+            jnp.concatenate([jnp.dot(abundance, sample, precision=WIDE), inner(sample, sample)])
         )
         target_w, gram_sample = both[:n_unit], both[n_unit:]
         unitig = unitig * target_w / jnp.dot(unitig, gram_sample, precision=HI)

time: 207 us -> 193 us (0.932)
  matrix products: 56.3 us -> 41.8 us
    dot_general x8, matrix products: 49.7 us -> 35.2 us  [the longest x6 19.9 us: inner(): lax.dot_general(left, right, (((0,), (0,)), ((), ())), precision=precisio...]
where the time goes in v1:
time: 193 us; the launch traced here: 192 us
  blocking collectives  109 us (56%)
  matrix products  41.8 us (22%)
  starting transfers between devices  14 us (7%)
  waiting for transfers between devices  14 us (7%)
  local copies, waits for them, and re-layouts  11.3 us (6%)
    all_to_all x4, blocking collectives, reduce_scatter(): return lax.all_to_all(chunks, axes, 0, 0, tiled=False).sum(0)  71.4 us
    all_to_all x3, blocking collectives, all_gather(): held = lax.all_to_all(copies, axes, 0, 0, tiled=False)  37.2 us
    dot_general x6, matrix products, inner(): lax.dot_general(left, right, (((0,), (0,)), ((), ())), precision=precisio...  19.9 us
    dot_general x2, matrix products, shards(): jnp.dot(abundance, sample, precision=WIDE)  15.3 us
    all_to_all x1, waiting for transfers between devices, all_gather(): held = lax.all_to_all(copies, axes, 0, 0, tiled=False)  12.9 us
    ppermute x2, starting transfers between devices, samp_sum(): return x + lax.ppermute(x, 'samp', [(0, 1), (1, 0)])  10.2 us
    unnamed x14, local copies, waits for them, and re-layouts  8.58 us
    dot_general x2, matrix products, shards(): sample = sample * target_h / jnp.dot(sample, gram_unit, precision=HI)  5.35 us
  transfers between devices with their start and end apart: 3, of which 3 were waited for; matrix products, arithmetic and copies ran while one was open for 2% of the time, Pallas kernels for 0%

profile of v1, /device:TPU:1, one launch (start us, length us, event | category | flops | bytes accessed | tf_op | source)
XLA Modules:
  0.0 191.9 jit_solution(5530327657622505324)
XLA Ops:
  0.6 2.3 %fusion.15 = f32[128,128]{1,0:T(8,128)S(1)} fusion(f32[1024,128]{1,0:T(8,128)} %param.4), kind=kOutput, calls=%fused_computation.23 | convolution fusion | flops 201326592 | bytes 589824 | tf_op jit(solution)/shard_map/dot_general | solution.py:15
  2.9 9.1 %fusion.14 = f32[2048,128]{1,0:T(8,128)S(1)} fusion(f32[1024,2048]{1,0:T(8,128)} %param.3, f32[1024,128]{1,0:T(8,128)S(1)} %copy-done), kind=kOutput, calls=%fused_computation.22 | convolution fusion | flops 1610612736 | bytes 9961472 | tf_op jit(solution)/shard_map/dot_general | solution.py:15
  12.1 24.3 %all_to_all.40 = f32[16,136,128]{2,1,0:T(8,128)S(1)} all-to-all(f32[16,136,128]{2,1,0:T(8,128)S(1)} %bitcast.40), channel_id=1, replica_groups=mesh['uz'=8,'uy'=4,'ux'=4,'samp'=2] {'uy','ux'}, dimensions={0} | all-to-all | bytes 2228224 | tf_op jit(solution)/shard_map/all_to_all | solution.py:22
  36.4 15.7 %all_to_all.41 = f32[8,17,128]{2,1,0:T(8,128)S(1)} all-to-all(f32[8,17,128]{2,1,0:T(8,128)S(1)} %reshape.27), channel_id=1, replica_groups=mesh['uz'=8,'uy'=4,'ux'=4,'samp'=2] {'uz'}, dimensions={0} | all-to-all | bytes 139264 | tf_op jit(solution)/shard_map/all_to_all | solution.py:22
  52.1 10.0 %all_to_all.42 = f32[8,17,128]{2,1,0:T(8,128)S(1)} all-to-all(f32[8,17,128]{2,1,0:T(8,128)S(1)} %broadcast_in_dim.12), channel_id=1, replica_groups=mesh['uz'=8,'uy'=4,'ux'=4,'samp'=2] {'uz'}, dimensions={0} | all-to-all | bytes 139264 | tf_op jit(solution)/shard_map/all_to_all | solution.py:27
  62.1 1.1 broadcast_in_dim.28
  63.1 3.8 %all-to-all-start.3 = ((f32[16,136,128]{2,1,0:T(8,128)}), f32[16,136,128]{2,1,0:T(8,128)S(1)}, u32[]{:S(2)}, u32[]{:S(2)}) async-start(f32[16,136,128]{2,1,0:T(8,128)} %broadcast_in_dim.28), calls=%async_computation.3 | async-start | bytes 2228224 | tf_op jit(solution)/shard_map/all_to_all | solution.py:27
  67.0 1.3 copy.15
  68.3 12.9 %all-to-all-done.3 = f32[16,136,128]{2,1,0:T(8,128)S(1)} async-done(((f32[16,136,128]{2,1,0:T(8,128)}), f32[16,136,128]{2,1,0:T(8,128)S(1)}, u32[]{:S(2)}, u32[]{:S(2)}) %all-to-all-start.3) | async-done | bytes 1114144 | tf_op jit(solution)/shard_map/all_to_all | solution.py:27
  81.2 1.3 copy.31
  82.6 3.0 %fusion = f32[2048,128]{0,1:T(8,128)S(1)} fusion(f32[2048,128]{1,0:T(8,128)} %param.5, f32[2048,128]{0,1:T(8,128)} %copy.15, f32[2048,128]{0,1:T(8,128)} %copy.31, f32[2176,128]{1,0:T(8,128)S(1)} %bitcast.39), kind=kOutput, calls=%fused_computation.2 | convolution fusion | flops 403177472 | bytes 4259840 | tf_op jit(solution)/shard_map/dot_general | solution.py:53
  86.5 7.6 %convolution_bitcast_fusion.4 = f32[1024,128]{0,1:T(8,128)S(1)} fusion(f32[2048,128]{0,1:T(8,128)S(1)} %fusion, f32[1024,2048]{1,0:T(8,128)} %param.3), kind=kOutput, calls=%fused_computation.6 | convolution fusion | flops 1610612736 | bytes 9961472 | tf_op jit(solution)/shard_map/dot_general | solution.py:55
  94.2 5.6 %collective-permute-start = (f32[1152,128]{0,1:T(8,128)S(1)}, f32[1152,128]{0,1:T(8,128)S(1)}, u32[]{:S(2)}, u32[]{:S(2)}) collective-permute-start(f32[1152,128]{0,1:T(8,128)S(1)} %pad_maximum_fusion.2), channel_id=1, source_target_pairs={{0,1},{1,0},{2,3},{3,2},{4,5},{5,4},{6,7},{7,6},{8,9},{9,8},{10,11... | collective-permute-start | bytes 1769480 | tf_op jit(solution)/shard_map/ppermute | solution.py:40
  103.1 6.0 %convolution_bitcast_fusion = f32[2048,128]{0,1:T(8,128)S(1)} fusion(f32[1024,128]{0,1:T(8,128)S(1)} %fusion.2, f32[1024,2048]{1,0:T(8,128)} %param.3), kind=kOutput, calls=%fused_computation | convolution fusion | flops 1610612736 | bytes 9961472 | tf_op jit(solution)/shard_map/dot_general | solution.py:15
  109.2 1.4 copy.19
  110.6 21.7 %all_to_all.43 = f32[16,136,128]{2,1,0:T(8,128)S(1)} all-to-all(f32[16,136,128]{2,1,0:T(8,128)} %bitcast.41), channel_id=1, replica_groups=mesh['uz'=8,'uy'=4,'ux'=4,'samp'=2] {'uy','ux'}, dimensions={0} | all-to-all | bytes 2228224 | tf_op jit(solution)/shard_map/all_to_all | solution.py:22
  132.3 9.8 %all_to_all.44 = f32[8,17,128]{2,1,0:T(8,128)S(1)} all-to-all(f32[8,17,128]{2,1,0:T(8,128)S(1)} %reshape.30), channel_id=1, replica_groups=mesh['uz'=8,'uy'=4,'ux'=4,'samp'=2] {'uz'}, dimensions={0} | all-to-all | bytes 139264 | tf_op jit(solution)/shard_map/all_to_all | solution.py:22
  142.2 10.1 %all_to_all.45 = f32[8,17,128]{2,1,0:T(8,128)S(1)} all-to-all(f32[8,17,128]{2,1,0:T(8,128)S(1)} %broadcast_in_dim.29), channel_id=1, replica_groups=mesh['uz'=8,'uy'=4,'ux'=4,'samp'=2] {'uz'}, dimensions={0} | all-to-all | bytes 139264 | tf_op jit(solution)/shard_map/all_to_all | solution.py:27
  152.3 17.2 %all_to_all.46 = f32[16,136,128]{2,1,0:T(8,128)S(1)} all-to-all(f32[16,136,128]{2,1,0:T(8,128)S(1)} %broadcast_in_dim.31), channel_id=1, replica_groups=mesh['uz'=8,'uy'=4,'ux'=4,'samp'=2] {'uy','ux'}, dimensions={0} | all-to-all | bytes 2228224 | tf_op jit(solution)/shard_map/all_to_all | solution.py:27
  170.6 1.3 copy.32
  171.9 2.4 %convolution_divide_fusion = f32[2048,128]{0,1:T(8,128)S(1)} fusion(f32[2048,128]{0,1:T(8,128)S(1)} %fusion, f32[2048,128]{0,1:T(8,128)} %copy.32, f32[2176,128]{1,0:T(8,128)} %bitcast.43), kind=kOutput, calls=%fused_computation.3 | convolution fusion | flops 403177472 | bytes 4259840 | tf_op jit(solution)/shard_map/dot_general | solution.py:53
  175.3 7.6 %convolution_bitcast_fusion.2 = f32[1024,128]{0,1:T(8,128)S(1)} fusion(f32[2048,128]{0,1:T(8,128)S(1)} %convolution_divide_fusion, f32[1024,2048]{1,0:T(8,128)} %param.3), kind=kOutput, calls=%fused_computation.4 | convolution fusion | flops 1610612736 | bytes 9961472 | tf_op jit(solution)/shard_map/dot_general | solution.py:55
  183.8 4.6 %collective-permute-start.1 = (f32[1152,128]{0,1:T(8,128)}, f32[1152,128]{0,1:T(8,128)S(1)}, u32[]{:S(2)}, u32[]{:S(2)}) collective-permute-start(f32[1152,128]{0,1:T(8,128)} %pad_maximum_fusion.3), channel_id=1, source_target_pairs={{0,1},{1,0},{2,3},{3,2},{4,5},{5,4},{6,7},{7,6},{8,9},{9,8},{10,11... | collective-permute-start | bytes 1769480 | tf_op jit(solution)/shard_map/ppermute | solution.py:40
  188.4 1.3 copy.25
  (36 shorter events, 9.9 us)
Async XLA Ops:
  0.6 2.3 %copy-start = (f32[1024,128]{1,0:T(8,128)S(1)}, f32[1024,128]{1,0:T(8,128)}, u32[]{:S(2)}) copy-start(f32[1024,128]{1,0:T(8,128)} %param.4) | copy-start | bytes 1572868
  63.1 3.8 %copy-start.2 = (f32[2048,128]{1,0:T(8,128)S(1)}, f32[2048,128]{1,0:T(8,128)}, u32[]{:S(2)}) copy-start(f32[2048,128]{1,0:T(8,128)} %param.5) | copy-start | bytes 3145732
  63.1 18.0 %all-to-all-start.3 = ((f32[16,136,128]{2,1,0:T(8,128)}), f32[16,136,128]{2,1,0:T(8,128)S(1)}, u32[]{:S(2)}, u32[]{:S(2)}) async-start(f32[16,136,128]{2,1,0:T(8,128)} %broadcast_in_dim.28), calls=%async_computation.3 | async-start | bytes 2228224 | tf_op jit(solution)/shard_map/all_to_all | solution.py:27
  94.2 7.2 %collective-permute-start = (f32[1152,128]{0,1:T(8,128)S(1)}, f32[1152,128]{0,1:T(8,128)S(1)}, u32[]{:S(2)}, u32[]{:S(2)}) collective-permute-start(f32[1152,128]{0,1:T(8,128)S(1)} %pad_maximum_fusion.2), channel_id=1, source_target_pairs={{0,1},{1,0},{2,3},{3,2},{4,5},{5,4},{6,7},{7,6},{8,9},{9,8},{10,11... | collective-permute-start | bytes 1769480 | tf_op jit(solution)/shard_map/ppermute | solution.py:40
  100.8 1.0 copy-start.3
  169.5 1.0 copy-start.1
  183.8 6.4 %collective-permute-start.1 = (f32[1152,128]{0,1:T(8,128)}, f32[1152,128]{0,1:T(8,128)S(1)}, u32[]{:S(2)}, u32[]{:S(2)}) collective-permute-start(f32[1152,128]{0,1:T(8,128)} %pad_maximum_fusion.3), channel_id=1, source_target_pairs={{0,1},{1,0},{2,3},{3,2},{4,5},{5,4},{6,7},{7,6},{8,9},{9,8},{10,11... | collective-permute-start | bytes 1769480 | tf_op jit(solution)/shard_map/ppermute | solution.py:40

commit v2 on v1

--- a/solution.py
+++ b/solution.py
@@ -28,10 +28,17 @@
     return held.reshape(n * piece.shape[0], *piece.shape[1:])
 
 
+def all_reduce(x, axes, n):
+    copies = jnp.broadcast_to(x[None], (n, *x.shape))
+    return lax.all_to_all(copies, axes, 0, 0, tiled=False).sum(0)
+
+
 def unit_sum(x, stages):
-    for axes, n in stages:
+    *outer, (last, n_last) = stages
+    for axes, n in outer:
         x = reduce_scatter(x, axes, n)
-    for axes, n in reversed(stages):
+    x = all_reduce(x, last, n_last)
+    for axes, n in reversed(outer):
         x = all_gather(x, axes, n)
     return x
 

time: 193 us -> 189 us (0.979)
  blocking collectives: 109 us -> 105 us
    all_to_all x0 -> x2, blocking collectives: none -> 42.3 us  [all_reduce(): return lax.all_to_all(copies, axes, 0, 0, tiled=False).sum(0)]
    all_to_all x4 -> x2, blocking collectives: 71.4 us -> 45.9 us  [reduce_scatter(): return lax.all_to_all(chunks, axes, 0, 0, tiled=False).sum(0)]
    all_to_all x3 -> x1, blocking collectives: 37.2 us -> 17 us  [all_gather(): held = lax.all_to_all(copies, axes, 0, 0, tiled=False)]
where the time goes in v2:
time: 189 us; the launch traced here: 188 us
  blocking collectives  105 us (56%)
  matrix products  41.8 us (22%)
  waiting for transfers between devices  14 us (7%)
  starting transfers between devices  13.7 us (7%)
  local copies, waits for them, and re-layouts  11.3 us (6%)
    all_to_all x2, blocking collectives, reduce_scatter(): return lax.all_to_all(chunks, axes, 0, 0, tiled=False).sum(0)  45.9 us
    all_to_all x2, blocking collectives, all_reduce(): return lax.all_to_all(copies, axes, 0, 0, tiled=False).sum(0)  42.3 us
    dot_general x6, matrix products, inner(): lax.dot_general(left, right, (((0,), (0,)), ((), ())), precision=precisio...  19.9 us
    all_to_all x1, blocking collectives, all_gather(): held = lax.all_to_all(copies, axes, 0, 0, tiled=False)  17 us
    dot_general x2, matrix products, shards(): jnp.dot(abundance, sample, precision=WIDE)  15.3 us
    all_to_all x1, waiting for transfers between devices, all_gather(): held = lax.all_to_all(copies, axes, 0, 0, tiled=False)  12.8 us
    ppermute x2, starting transfers between devices, samp_sum(): return x + lax.ppermute(x, 'samp', [(0, 1), (1, 0)])  9.91 us
    unnamed x14, local copies, waits for them, and re-layouts  8.58 us
  transfers between devices with their start and end apart: 3, of which 3 were waited for; matrix products, arithmetic and copies ran while one was open for 2% of the time, Pallas kernels for 0%

profile of v2, /device:TPU:1, one launch (start us, length us, event | category | flops | bytes accessed | tf_op | source)
XLA Modules:
  0.0 188.2 jit_solution(16779663314059039335)
XLA Ops:
  0.6 2.3 %fusion.15 = f32[128,128]{1,0:T(8,128)S(1)} fusion(f32[1024,128]{1,0:T(8,128)} %param.4), kind=kOutput, calls=%fused_computation.23 | convolution fusion | flops 201326592 | bytes 589824 | tf_op jit(solution)/shard_map/dot_general | solution.py:15
  2.9 9.1 %fusion.14 = f32[2048,128]{1,0:T(8,128)S(1)} fusion(f32[1024,2048]{1,0:T(8,128)} %param.3, f32[1024,128]{1,0:T(8,128)S(1)} %copy-done), kind=kOutput, calls=%fused_computation.22 | convolution fusion | flops 1610612736 | bytes 9961472 | tf_op jit(solution)/shard_map/dot_general | solution.py:15
  12.1 24.3 %all_to_all.30 = f32[16,136,128]{2,1,0:T(8,128)S(1)} all-to-all(f32[16,136,128]{2,1,0:T(8,128)S(1)} %bitcast.40), channel_id=1, replica_groups=mesh['uz'=8,'uy'=4,'ux'=4,'samp'=2] {'uy','ux'}, dimensions={0} | all-to-all | bytes 2228224 | tf_op jit(solution)/shard_map/all_to_all | solution.py:22
  36.4 23.2 %all_to_all.31 = f32[8,136,128]{2,1,0:T(8,128)S(1)} all-to-all(f32[8,136,128]{2,1,0:T(8,128)S(1)} %broadcast_in_dim.8), channel_id=1, replica_groups=mesh['uz'=8,'uy'=4,'ux'=4,'samp'=2] {'uz'}, dimensions={0} | all-to-all | bytes 1114112 | tf_op jit(solution)/shard_map/all_to_all | solution.py:33
  59.6 1.1 broadcast_in_dim.9
  60.7 3.8 %all-to-all-start.2 = ((f32[16,136,128]{2,1,0:T(8,128)}), f32[16,136,128]{2,1,0:T(8,128)S(1)}, u32[]{:S(2)}, u32[]{:S(2)}) async-start(f32[16,136,128]{2,1,0:T(8,128)} %broadcast_in_dim.9), calls=%async_computation.2 | async-start | bytes 2228224 | tf_op jit(solution)/shard_map/all_to_all | solution.py:27
  64.6 1.3 copy.27
  65.9 12.8 %all-to-all-done.2 = f32[16,136,128]{2,1,0:T(8,128)S(1)} async-done(((f32[16,136,128]{2,1,0:T(8,128)}), f32[16,136,128]{2,1,0:T(8,128)S(1)}, u32[]{:S(2)}, u32[]{:S(2)}) %all-to-all-start.2) | async-done | bytes 1114144 | tf_op jit(solution)/shard_map/all_to_all | solution.py:27
  78.7 1.3 copy.43
  80.1 3.0 %fusion = f32[2048,128]{0,1:T(8,128)S(1)} fusion(f32[2048,128]{1,0:T(8,128)} %param.5, f32[2048,128]{0,1:T(8,128)} %copy.27, f32[2048,128]{0,1:T(8,128)} %copy.43, f32[2176,128]{1,0:T(8,128)S(1)} %bitcast.39), kind=kOutput, calls=%fused_computation.2 | convolution fusion | flops 403177472 | bytes 4259840 | tf_op jit(solution)/shard_map/dot_general | solution.py:60
  84.0 7.6 %convolution_bitcast_fusion.4 = f32[1024,128]{0,1:T(8,128)S(1)} fusion(f32[2048,128]{0,1:T(8,128)S(1)} %fusion, f32[1024,2048]{1,0:T(8,128)} %param.3), kind=kOutput, calls=%fused_computation.6 | convolution fusion | flops 1610612736 | bytes 9961472 | tf_op jit(solution)/shard_map/dot_general | solution.py:62
  91.7 5.5 %collective-permute-start = (f32[1152,128]{0,1:T(8,128)S(1)}, f32[1152,128]{0,1:T(8,128)S(1)}, u32[]{:S(2)}, u32[]{:S(2)}) collective-permute-start(f32[1152,128]{0,1:T(8,128)S(1)} %pad_maximum_fusion.2), channel_id=1, source_target_pairs={{0,1},{1,0},{2,3},{3,2},{4,5},{5,4},{6,7},{7,6},{8,9},{9,8},{10,11... | collective-permute-start | bytes 1769480 | tf_op jit(solution)/shard_map/ppermute | solution.py:47
  97.2 1.0 copy.29
  100.5 6.0 %convolution_bitcast_fusion = f32[2048,128]{0,1:T(8,128)S(1)} fusion(f32[1024,128]{0,1:T(8,128)S(1)} %fusion.2, f32[1024,2048]{1,0:T(8,128)} %param.3), kind=kOutput, calls=%fused_computation | convolution fusion | flops 1610612736 | bytes 9961472 | tf_op jit(solution)/shard_map/dot_general | solution.py:15
  106.6 1.4 copy.31
  108.0 21.7 %all_to_all.32 = f32[16,136,128]{2,1,0:T(8,128)S(1)} all-to-all(f32[16,136,128]{2,1,0:T(8,128)} %bitcast.41), channel_id=1, replica_groups=mesh['uz'=8,'uy'=4,'ux'=4,'samp'=2] {'uy','ux'}, dimensions={0} | all-to-all | bytes 2228224 | tf_op jit(solution)/shard_map/all_to_all | solution.py:22
  129.7 19.1 %all_to_all.33 = f32[8,136,128]{2,1,0:T(8,128)S(1)} all-to-all(f32[8,136,128]{2,1,0:T(8,128)S(1)} %broadcast_in_dim.10), channel_id=1, replica_groups=mesh['uz'=8,'uy'=4,'ux'=4,'samp'=2] {'uz'}, dimensions={0} | all-to-all | bytes 1114112 | tf_op jit(solution)/shard_map/all_to_all | solution.py:33
  149.0 17.0 %all_to_all.34 = f32[16,136,128]{2,1,0:T(8,128)S(1)} all-to-all(f32[16,136,128]{2,1,0:T(8,128)S(1)} %broadcast_in_dim.11), channel_id=1, replica_groups=mesh['uz'=8,'uy'=4,'ux'=4,'samp'=2] {'uy','ux'}, dimensions={0} | all-to-all | bytes 2228224 | tf_op jit(solution)/shard_map/all_to_all | solution.py:27
  167.1 1.3 copy.44
  168.4 2.4 %convolution_divide_fusion = f32[2048,128]{0,1:T(8,128)S(1)} fusion(f32[2048,128]{0,1:T(8,128)S(1)} %fusion, f32[2048,128]{0,1:T(8,128)} %copy.44, f32[2176,128]{1,0:T(8,128)} %bitcast.43), kind=kOutput, calls=%fused_computation.3 | convolution fusion | flops 403177472 | bytes 4259840 | tf_op jit(solution)/shard_map/dot_general | solution.py:60
  171.8 7.6 %convolution_bitcast_fusion.2 = f32[1024,128]{0,1:T(8,128)S(1)} fusion(f32[2048,128]{0,1:T(8,128)S(1)} %convolution_divide_fusion, f32[1024,2048]{1,0:T(8,128)} %param.3), kind=kOutput, calls=%fused_computation.4 | convolution fusion | flops 1610612736 | bytes 9961472 | tf_op jit(solution)/shard_map/dot_general | solution.py:62
  180.3 4.4 %collective-permute-start.1 = (f32[1152,128]{0,1:T(8,128)}, f32[1152,128]{0,1:T(8,128)S(1)}, u32[]{:S(2)}, u32[]{:S(2)}) collective-permute-start(f32[1152,128]{0,1:T(8,128)} %pad_maximum_fusion.3), channel_id=1, source_target_pairs={{0,1},{1,0},{2,3},{3,2},{4,5},{5,4},{6,7},{7,6},{8,9},{9,8},{10,11... | collective-permute-start | bytes 1769480 | tf_op jit(solution)/shard_map/ppermute | solution.py:47
  184.7 1.3 copy.37
  187.2 1.0 copy.36
  (30 shorter events, 7.9 us)
Async XLA Ops:
  0.6 2.3 %copy-start = (f32[1024,128]{1,0:T(8,128)S(1)}, f32[1024,128]{1,0:T(8,128)}, u32[]{:S(2)}) copy-start(f32[1024,128]{1,0:T(8,128)} %param.4) | copy-start | bytes 1572868
  60.7 3.8 %copy-start.2 = (f32[2048,128]{1,0:T(8,128)S(1)}, f32[2048,128]{1,0:T(8,128)}, u32[]{:S(2)}) copy-start(f32[2048,128]{1,0:T(8,128)} %param.5) | copy-start | bytes 3145732
  60.7 18.0 %all-to-all-start.2 = ((f32[16,136,128]{2,1,0:T(8,128)}), f32[16,136,128]{2,1,0:T(8,128)S(1)}, u32[]{:S(2)}, u32[]{:S(2)}) async-start(f32[16,136,128]{2,1,0:T(8,128)} %broadcast_in_dim.9), calls=%async_computation.2 | async-start | bytes 2228224 | tf_op jit(solution)/shard_map/all_to_all | solution.py:27
  91.7 7.1 %collective-permute-start = (f32[1152,128]{0,1:T(8,128)S(1)}, f32[1152,128]{0,1:T(8,128)S(1)}, u32[]{:S(2)}, u32[]{:S(2)}) collective-permute-start(f32[1152,128]{0,1:T(8,128)S(1)} %pad_maximum_fusion.2), channel_id=1, source_target_pairs={{0,1},{1,0},{2,3},{3,2},{4,5},{5,4},{6,7},{7,6},{8,9},{9,8},{10,11... | collective-permute-start | bytes 1769480 | tf_op jit(solution)/shard_map/ppermute | solution.py:47
  98.2 1.0 copy-start.3
  166.0 1.0 copy-start.1
  180.3 6.3 %collective-permute-start.1 = (f32[1152,128]{0,1:T(8,128)}, f32[1152,128]{0,1:T(8,128)S(1)}, u32[]{:S(2)}, u32[]{:S(2)}) collective-permute-start(f32[1152,128]{0,1:T(8,128)} %pad_maximum_fusion.3), channel_id=1, source_target_pairs={{0,1},{1,0},{2,3},{3,2},{4,5},{5,4},{6,7},{7,6},{8,9},{9,8},{10,11... | collective-permute-start | bytes 1769480 | tf_op jit(solution)/shard_map/ppermute | solution.py:47

commit v3 on v2

--- a/solution.py
+++ b/solution.py
@@ -7,7 +7,7 @@
 ITERS = 2
 
 
-HI = lax.Precision.HIGHEST
+HI = lax.Precision.HIGH
 WIDE = lax.Precision.HIGH
 
 

time: 189 us -> 186 us (0.984)
  matrix products: 41.8 us -> 39 us
where the time goes in v3:
time: 186 us; the launch traced here: 185 us
  blocking collectives  105 us (56%)
  matrix products  39 us (21%)
  waiting for transfers between devices  14 us (8%)
  starting transfers between devices  13.7 us (7%)
  local copies, waits for them, and re-layouts  11.3 us (6%)
    all_to_all x2, blocking collectives, reduce_scatter(): return lax.all_to_all(chunks, axes, 0, 0, tiled=False).sum(0)  45.9 us
    all_to_all x2, blocking collectives, all_reduce(): return lax.all_to_all(copies, axes, 0, 0, tiled=False).sum(0)  42.3 us
    dot_general x6, matrix products, inner(): lax.dot_general(left, right, (((0,), (0,)), ((), ())), precision=precisio...  18.5 us
    all_to_all x1, blocking collectives, all_gather(): held = lax.all_to_all(copies, axes, 0, 0, tiled=False)  17 us
    dot_general x2, matrix products, shards(): jnp.dot(abundance, sample, precision=WIDE)  15.3 us
    all_to_all x1, waiting for transfers between devices, all_gather(): held = lax.all_to_all(copies, axes, 0, 0, tiled=False)  12.8 us
    ppermute x2, starting transfers between devices, samp_sum(): return x + lax.ppermute(x, 'samp', [(0, 1), (1, 0)])  9.89 us
    unnamed x14, local copies, waits for them, and re-layouts  8.58 us
  transfers between devices with their start and end apart: 3, of which 3 were waited for; matrix products, arithmetic and copies ran while one was open for 2% of the time, Pallas kernels for 0%

profile of v3, /device:TPU:1, one launch (start us, length us, event | category | flops | bytes accessed | tf_op | source)
XLA Modules:
  0.0 185.5 jit_solution(1124200871537789141)
XLA Ops:
  0.6 1.8 fusion.15
  2.5 9.1 %fusion.14 = f32[2048,128]{1,0:T(8,128)S(1)} fusion(f32[1024,2048]{1,0:T(8,128)} %param.3, f32[1024,128]{1,0:T(8,128)S(1)} %copy-done), kind=kOutput, calls=%fused_computation.22 | convolution fusion | flops 1610612736 | bytes 9961472 | tf_op jit(solution)/shard_map/dot_general | solution.py:15
  11.7 24.3 %all_to_all.30 = f32[16,136,128]{2,1,0:T(8,128)S(1)} all-to-all(f32[16,136,128]{2,1,0:T(8,128)S(1)} %bitcast.40), channel_id=1, replica_groups=mesh['uz'=8,'uy'=4,'ux'=4,'samp'=2] {'uy','ux'}, dimensions={0} | all-to-all | bytes 2228224 | tf_op jit(solution)/shard_map/all_to_all | solution.py:22
  36.0 23.2 %all_to_all.31 = f32[8,136,128]{2,1,0:T(8,128)S(1)} all-to-all(f32[8,136,128]{2,1,0:T(8,128)S(1)} %broadcast_in_dim.8), channel_id=1, replica_groups=mesh['uz'=8,'uy'=4,'ux'=4,'samp'=2] {'uz'}, dimensions={0} | all-to-all | bytes 1114112 | tf_op jit(solution)/shard_map/all_to_all | solution.py:33
  59.2 1.1 broadcast_in_dim.9
  60.3 3.8 %all-to-all-start.2 = ((f32[16,136,128]{2,1,0:T(8,128)}), f32[16,136,128]{2,1,0:T(8,128)S(1)}, u32[]{:S(2)}, u32[]{:S(2)}) async-start(f32[16,136,128]{2,1,0:T(8,128)} %broadcast_in_dim.9), calls=%async_computation.2 | async-start | bytes 2228224 | tf_op jit(solution)/shard_map/all_to_all | solution.py:27
  64.1 1.3 copy.27
  65.5 12.8 %all-to-all-done.2 = f32[16,136,128]{2,1,0:T(8,128)S(1)} async-done(((f32[16,136,128]{2,1,0:T(8,128)}), f32[16,136,128]{2,1,0:T(8,128)S(1)}, u32[]{:S(2)}, u32[]{:S(2)}) %all-to-all-start.2) | async-done | bytes 1114144 | tf_op jit(solution)/shard_map/all_to_all | solution.py:27
  78.3 1.3 copy.43
  79.7 2.5 %fusion = f32[2048,128]{0,1:T(8,128)S(1)} fusion(f32[2048,128]{1,0:T(8,128)} %param.5, f32[2048,128]{0,1:T(8,128)} %copy.27, f32[2048,128]{0,1:T(8,128)} %copy.43, f32[2176,128]{1,0:T(8,128)S(1)} %bitcast.39), kind=kOutput, calls=%fused_computation.2 | convolution fusion | flops 201850880 | bytes 4259840 | tf_op jit(solution)/shard_map/dot_general | solution.py:60
  82.8 7.7 %convolution_bitcast_fusion.4 = f32[1024,128]{0,1:T(8,128)S(1)} fusion(f32[2048,128]{0,1:T(8,128)S(1)} %fusion, f32[1024,2048]{1,0:T(8,128)} %param.3), kind=kOutput, calls=%fused_computation.6 | convolution fusion | flops 1610612736 | bytes 9961472 | tf_op jit(solution)/shard_map/dot_general | solution.py:62
  90.5 5.5 %collective-permute-start = (f32[1152,128]{0,1:T(8,128)S(1)}, f32[1152,128]{0,1:T(8,128)S(1)}, u32[]{:S(2)}, u32[]{:S(2)}) collective-permute-start(f32[1152,128]{0,1:T(8,128)S(1)} %pad_maximum_fusion.2), channel_id=1, source_target_pairs={{0,1},{1,0},{2,3},{3,2},{4,5},{5,4},{6,7},{7,6},{8,9},{9,8},{10,11... | collective-permute-start | bytes 1769480 | tf_op jit(solution)/shard_map/ppermute | solution.py:47
  96.0 1.0 copy.29
  98.8 6.0 %convolution_bitcast_fusion = f32[2048,128]{0,1:T(8,128)S(1)} fusion(f32[1024,128]{0,1:T(8,128)S(1)} %fusion.2, f32[1024,2048]{1,0:T(8,128)} %param.3), kind=kOutput, calls=%fused_computation | convolution fusion | flops 1610612736 | bytes 9961472 | tf_op jit(solution)/shard_map/dot_general | solution.py:15
  104.9 1.4 copy.31
  106.3 21.7 %all_to_all.32 = f32[16,136,128]{2,1,0:T(8,128)S(1)} all-to-all(f32[16,136,128]{2,1,0:T(8,128)} %bitcast.41), channel_id=1, replica_groups=mesh['uz'=8,'uy'=4,'ux'=4,'samp'=2] {'uy','ux'}, dimensions={0} | all-to-all | bytes 2228224 | tf_op jit(solution)/shard_map/all_to_all | solution.py:22
  128.1 19.1 %all_to_all.33 = f32[8,136,128]{2,1,0:T(8,128)S(1)} all-to-all(f32[8,136,128]{2,1,0:T(8,128)S(1)} %broadcast_in_dim.10), channel_id=1, replica_groups=mesh['uz'=8,'uy'=4,'ux'=4,'samp'=2] {'uz'}, dimensions={0} | all-to-all | bytes 1114112 | tf_op jit(solution)/shard_map/all_to_all | solution.py:33
  147.3 17.0 %all_to_all.34 = f32[16,136,128]{2,1,0:T(8,128)S(1)} all-to-all(f32[16,136,128]{2,1,0:T(8,128)S(1)} %broadcast_in_dim.11), channel_id=1, replica_groups=mesh['uz'=8,'uy'=4,'ux'=4,'samp'=2] {'uy','ux'}, dimensions={0} | all-to-all | bytes 2228224 | tf_op jit(solution)/shard_map/all_to_all | solution.py:27
  165.4 1.3 copy.44
  166.7 1.9 %convolution_divide_fusion = f32[2048,128]{0,1:T(8,128)S(1)} fusion(f32[2048,128]{0,1:T(8,128)S(1)} %fusion, f32[2048,128]{0,1:T(8,128)} %copy.44, f32[2176,128]{1,0:T(8,128)} %bitcast.43), kind=kOutput, calls=%fused_computation.3 | convolution fusion | flops 201850880 | bytes 4259840 | tf_op jit(solution)/shard_map/dot_general | solution.py:60
  169.2 7.6 %convolution_bitcast_fusion.2 = f32[1024,128]{0,1:T(8,128)S(1)} fusion(f32[2048,128]{0,1:T(8,128)S(1)} %convolution_divide_fusion, f32[1024,2048]{1,0:T(8,128)} %param.3), kind=kOutput, calls=%fused_computation.4 | convolution fusion | flops 1610612736 | bytes 9961472 | tf_op jit(solution)/shard_map/dot_general | solution.py:62
  177.8 4.4 %collective-permute-start.1 = (f32[1152,128]{0,1:T(8,128)}, f32[1152,128]{0,1:T(8,128)S(1)}, u32[]{:S(2)}, u32[]{:S(2)}) collective-permute-start(f32[1152,128]{0,1:T(8,128)} %pad_maximum_fusion.3), channel_id=1, source_target_pairs={{0,1},{1,0},{2,3},{3,2},{4,5},{5,4},{6,7},{7,6},{8,9},{9,8},{10,11... | collective-permute-start | bytes 1769480 | tf_op jit(solution)/shard_map/ppermute | solution.py:47
  182.2 1.3 copy.37
  184.5 1.0 copy.36
  (30 shorter events, 6.5 us)
Async XLA Ops:
  0.6 1.9 %copy-start = (f32[1024,128]{1,0:T(8,128)S(1)}, f32[1024,128]{1,0:T(8,128)}, u32[]{:S(2)}) copy-start(f32[1024,128]{1,0:T(8,128)} %param.4) | copy-start | bytes 1572868
  60.3 3.8 %copy-start.2 = (f32[2048,128]{1,0:T(8,128)S(1)}, f32[2048,128]{1,0:T(8,128)}, u32[]{:S(2)}) copy-start(f32[2048,128]{1,0:T(8,128)} %param.5) | copy-start | bytes 3145732
  60.3 18.0 %all-to-all-start.2 = ((f32[16,136,128]{2,1,0:T(8,128)}), f32[16,136,128]{2,1,0:T(8,128)S(1)}, u32[]{:S(2)}, u32[]{:S(2)}) async-start(f32[16,136,128]{2,1,0:T(8,128)} %broadcast_in_dim.9), calls=%async_computation.2 | async-start | bytes 2228224 | tf_op jit(solution)/shard_map/all_to_all | solution.py:27
  90.5 7.1 %collective-permute-start = (f32[1152,128]{0,1:T(8,128)S(1)}, f32[1152,128]{0,1:T(8,128)S(1)}, u32[]{:S(2)}, u32[]{:S(2)}) collective-permute-start(f32[1152,128]{0,1:T(8,128)S(1)} %pad_maximum_fusion.2), channel_id=1, source_target_pairs={{0,1},{1,0},{2,3},{3,2},{4,5},{5,4},{6,7},{7,6},{8,9},{9,8},{10,11... | collective-permute-start | bytes 1769480 | tf_op jit(solution)/shard_map/ppermute | solution.py:47
  97.0 1.0 copy-start.3
  164.3 1.0 copy-start.1
  177.8 6.3 %collective-permute-start.1 = (f32[1152,128]{0,1:T(8,128)}, f32[1152,128]{0,1:T(8,128)S(1)}, u32[]{:S(2)}, u32[]{:S(2)}) collective-permute-start(f32[1152,128]{0,1:T(8,128)} %pad_maximum_fusion.3), channel_id=1, source_target_pairs={{0,1},{1,0},{2,3},{3,2},{4,5},{5,4},{6,7},{7,6},{8,9},{9,8},{10,11... | collective-permute-start | bytes 1769480 | tf_op jit(solution)/shard_map/ppermute | solution.py:47

commit v4 on v3

--- a/solution.py
+++ b/solution.py
@@ -47,23 +47,29 @@
     return x + lax.ppermute(x, "samp", [(0, 1), (1, 0)])
 
 
+def dot(spec, left, right):
+    return jnp.einsum(spec, left, right, precision=HI, preferred_element_type=jnp.float32)
+
+
 def shards(stages, abundance, unitig_factor, sample_factor):
-    unitig = unitig_factor
-    sample = sample_factor
-    n_samp = sample.shape[0]
-    n_unit = unitig.shape[0]
+    n = stages[0][1]
+    rows, k = sample_factor.shape
+    wide = abundance.reshape(abundance.shape[0], n, rows // n)
+    unitig = unitig_factor.T
+    sample = sample_factor.reshape(n, rows // n, k).transpose(0, 2, 1)
     for sweep in range(ITERS):
-        both = unit_sum(
-            jnp.concatenate([inner(abundance, unitig, WIDE), inner(unitig, unitig)]), stages
-        )
-        target_h, gram_unit = both[:n_samp], both[n_samp:]
-        sample = sample * target_h / jnp.dot(sample, gram_unit, precision=HI)
-        both = samp_sum(
-            jnp.concatenate([jnp.dot(abundance, sample, precision=WIDE), inner(sample, sample)])
-        )
-        target_w, gram_sample = both[:n_unit], both[n_unit:]
-        unitig = unitig * target_w / jnp.dot(unitig, gram_sample, precision=HI)
-    return (unitig, sample)
+        gram_unit = dot("ku,lu->kl", unitig, unitig)
+        target_h = dot("ku,ujs->jks", unitig, wide)
+        width = rows // n
+        both = jnp.concatenate([target_h, gram_unit.reshape(n, -1, width)], axis=1)
+        both = unit_sum(both.reshape(-1, width), stages).reshape(n, -1, width)
+        target_h, gram_unit = both[:, :k], both[:, k:].reshape(k, k)
+        sample = sample * target_h / dot("kl,jks->jls", gram_unit, sample)
+        gram_sample = dot("jks,jls->kl", sample, sample)
+        both = samp_sum(jnp.concatenate([dot("jks,ujs->ku", sample, wide), gram_sample], axis=1))
+        target_w, gram_sample = both[:, : unitig.shape[1]], both[:, unitig.shape[1] :]
+        unitig = unitig * target_w / dot("kl,ku->lu", gram_sample, unitig)
+    return (unitig.T, sample.transpose(0, 2, 1).reshape(rows, k))
 
 
 def unit_dims(mesh):

time: 186 us -> 179 us (0.962)
  blocking collectives: 105 us -> 120 us
  waiting for transfers between devices: 14 us -> 2.47 us
  local copies, waits for them, and re-layouts: 11.3 us -> 6.02 us
  starting transfers between devices: 13.7 us -> 10.2 us
  matrix products: 39 us -> 35.7 us
    all_to_all x1 -> x2, blocking collectives: 17 us -> 34.2 us  [all_gather(): held = lax.all_to_all(copies, axes, 0, 0, tiled=False)]
    all_to_all x1 -> x0, waiting for transfers between devices: 12.8 us -> none  [all_gather(): held = lax.all_to_all(copies, axes, 0, 0, tiled=False)]
    dot_general x12 -> x11, matrix products: 39 us -> 35.1 us  [dot(): jnp.einsum(spec, left, right, precision=HI, preferred_element_type=jnp.fl...]
    all_to_all x1 -> x0, starting transfers between devices: 3.83 us -> none  [all_gather(): held = lax.all_to_all(copies, axes, 0, 0, tiled=False)]
    unnamed x14 -> x12, local copies, waits for them, and re-layouts: 8.58 us -> 5.61 us
  transfers between devices with their start and end apart: 3 -> 2, of which waited for: 3 -> 2; matrix products, arithmetic and copies ran while one was open for 2% -> 1% of each run, Pallas kernels for 0% -> 0%
where the time goes in v4:
time: 179 us; the launch traced here: 178 us
  blocking collectives  120 us (67%)
  matrix products  35.7 us (20%)
  starting transfers between devices  10.2 us (6%)
  local copies, waits for them, and re-layouts  6.02 us (3%)
  other arithmetic  2.94 us (2%)
  waiting for transfers between devices  2.47 us (1%)
    all_to_all x2, blocking collectives, reduce_scatter(): return lax.all_to_all(chunks, axes, 0, 0, tiled=False).sum(0)  44.3 us
    all_to_all x2, blocking collectives, all_reduce(): return lax.all_to_all(copies, axes, 0, 0, tiled=False).sum(0)  41.7 us
    dot_general x11, matrix products, dot(): jnp.einsum(spec, left, right, precision=HI, preferred_element_type=jnp.fl...  35.1 us
    all_to_all x2, blocking collectives, all_gather(): held = lax.all_to_all(copies, axes, 0, 0, tiled=False)  34.2 us
    ppermute x2, starting transfers between devices, samp_sum(): return x + lax.ppermute(x, 'samp', [(0, 1), (1, 0)])  10.2 us
    unnamed x12, local copies, waits for them, and re-layouts  5.61 us
  transfers between devices with their start and end apart: 2, of which 2 were waited for; matrix products, arithmetic and copies ran while one was open for 1% of the time, Pallas kernels for 0%

profile of v4, /device:TPU:1, one launch (start us, length us, event | category | flops | bytes accessed | tf_op | source)
XLA Modules:
  0.0 178.4 jit_solution(11503973325732591747)
XLA Ops:
  0.6 1.8 %convolution_bitcast_fusion.4 = f32[16,8,128]{2,1,0:T(8,128)S(1)} fusion(f32[1024,128]{1,0:T(8,128)} %param.4), kind=kOutput, calls=%fused_computation.21 | convolution fusion | flops 100663296 | bytes 589824 | tf_op jit(solution)/shard_map/ku,lu->kl/dot_general | solution.py:51
  2.5 5.6 %fusion.12 = f32[16,128,128]{2,1,0:T(8,128)S(1)} fusion(f32[1024,128]{1,0:T(8,128)} %param.4, f32[1024,2048]{1,0:T(8,128)} %param.3), kind=kOutput, calls=%fused_computation.12 | convolution fusion | flops 1610612736 | bytes 9961472 | tf_op jit(solution)/shard_map/ku,ujs->jks/dot_general | solution.py:51
  8.2 24.4 %all_to_all.30 = f32[16,136,128]{2,1,0:T(8,128)S(1)} all-to-all(f32[16,136,128]{2,1,0:T(8,128)S(1)} %pad_maximum_fusion), channel_id=1, replica_groups=mesh['uz'=8,'uy'=4,'ux'=4,'samp'=2] {'uy','ux'}, dimensions={0} | all-to-all | bytes 2228224 | tf_op jit(solution)/shard_map/all_to_all | solution.py:22
  32.7 23.2 %all_to_all.31 = f32[8,136,128]{2,1,0:T(8,128)S(1)} all-to-all(f32[8,136,128]{2,1,0:T(8,128)S(1)} %broadcast_in_dim.8), channel_id=1, replica_groups=mesh['uz'=8,'uy'=4,'ux'=4,'samp'=2] {'uz'}, dimensions={0} | all-to-all | bytes 1114112 | tf_op jit(solution)/shard_map/all_to_all | solution.py:33
  56.0 16.6 %all_to_all.32 = f32[16,136,128]{2,1,0:T(8,128)S(1)} all-to-all(f32[16,136,128]{2,1,0:T(8,128)S(1)} %broadcast_in_dim.9), channel_id=1, replica_groups=mesh['uz'=8,'uy'=4,'ux'=4,'samp'=2] {'uy','ux'}, dimensions={0} | all-to-all | bytes 2228224 | tf_op jit(solution)/shard_map/all_to_all | solution.py:27
  72.7 1.3 copy.84
  74.6 1.6 multiply_divide_fusion
  76.1 1.0 convolution_bitcast_fusion.3
  77.1 7.7 %fusion.19 = f32[128,1024]{1,0:T(8,128)S(1)} fusion(f32[16,128,128]{1,2,0:T(8,128)S(1)} %multiply_divide_fusion, f32[1024,2048]{1,0:T(8,128)} %param.3), kind=kOutput, calls=%fused_computation.16 | convolution fusion | flops 1610612736 | bytes 9961472 | tf_op jit(solution)/shard_map/jks,ujs->ku/dot_general | solution.py:51
  85.7 5.1 %collective-permute-start = (f32[128,1152]{1,0:T(8,128)}, f32[128,1152]{1,0:T(8,128)S(1)}, u32[]{:S(2)}, u32[]{:S(2)}) collective-permute-start(f32[128,1152]{1,0:T(8,128)} %pad_maximum_fusion.2), channel_id=1, source_target_pairs={{0,1},{1,0},{2,3},{3,2},{4,5},{5,4},{6,7},{7,6},{8,9},{9,8},{10,11... | collective-permute-start | bytes 1769480 | tf_op jit(solution)/shard_map/ppermute | solution.py:47
  90.9 1.0 copy.55
  92.8 1.5 fusion.29
  94.6 6.0 %fusion.15 = f32[16,128,128]{2,1,0:T(8,128)S(1)} fusion(f32[128,1024]{1,0:T(8,128)S(1)} %fusion.29, f32[1024,2048]{1,0:T(8,128)} %param.3), kind=kOutput, calls=%fused_computation.13 | convolution fusion | flops 1610612736 | bytes 9961472 | tf_op jit(solution)/shard_map/ku,ujs->jks/dot_general | solution.py:51
  100.8 19.9 %all_to_all.33 = f32[16,136,128]{2,1,0:T(8,128)S(1)} all-to-all(f32[16,136,128]{2,1,0:T(8,128)S(1)} %pad_maximum_fusion.1), channel_id=1, replica_groups=mesh['uz'=8,'uy'=4,'ux'=4,'samp'=2] {'uy','ux'}, dimensions={0} | all-to-all | bytes 2228224 | tf_op jit(solution)/shard_map/all_to_all | solution.py:22
  120.8 18.6 %all_to_all.34 = f32[8,136,128]{2,1,0:T(8,128)S(1)} all-to-all(f32[8,136,128]{2,1,0:T(8,128)S(1)} %broadcast_in_dim.10), channel_id=1, replica_groups=mesh['uz'=8,'uy'=4,'ux'=4,'samp'=2] {'uz'}, dimensions={0} | all-to-all | bytes 1114112 | tf_op jit(solution)/shard_map/all_to_all | solution.py:33
  139.5 17.6 %all_to_all.35 = f32[16,136,128]{2,1,0:T(8,128)S(1)} all-to-all(f32[16,136,128]{2,1,0:T(8,128)S(1)} %broadcast_in_dim.11), channel_id=1, replica_groups=mesh['uz'=8,'uy'=4,'ux'=4,'samp'=2] {'uy','ux'}, dimensions={0} | all-to-all | bytes 2228224 | tf_op jit(solution)/shard_map/all_to_all | solution.py:27
  157.1 1.0 copy-done.2
  158.2 1.3 copy.85
  159.5 1.8 %fusion.18 = f32[16,128,128]{1,2,0:T(8,128)S(1)} fusion(f32[16,128,128]{1,2,0:T(8,128)S(1)} %multiply_divide_fusion, f32[16,128,128]{1,2,0:T(8,128)} %copy.85, f32[16,136,128]{2,1,0:T(8,128)} %copy-done.2), kind=kOutput, calls=%fused_computation.15 | convolution fusion | flops 201850880 | bytes 4259840 | tf_op jit(solution)/shard_map/kl,jks->jls/dot_general | solution.py:51
  161.3 1.0 convolution_bitcast_fusion.1
  162.3 7.7 %fusion.22 = f32[128,1024]{1,0:T(8,128)S(1)} fusion(f32[16,128,128]{1,2,0:T(8,128)S(1)} %fusion.18, f32[1024,2048]{1,0:T(8,128)} %param.3), kind=kOutput, calls=%fused_computation.17 | convolution fusion | flops 1610612736 | bytes 9961472 | tf_op jit(solution)/shard_map/jks,ujs->ku/dot_general | solution.py:51
  170.1 5.1 %collective-permute-start.1 = (f32[128,1152]{1,0:T(8,128)S(1)}, f32[128,1152]{1,0:T(8,128)S(1)}, u32[]{:S(2)}, u32[]{:S(2)}) collective-permute-start(f32[128,1152]{1,0:T(8,128)S(1)} %pad_maximum_fusion.3), channel_id=1, source_target_pairs={{0,1},{1,0},{2,3},{3,2},{4,5},{5,4},{6,7},{7,6},{8,9},{9,8},{10,11... | collective-permute-start | bytes 1769480 | tf_op jit(solution)/shard_map/ppermute | solution.py:47
  175.2 1.6 collective-permute-done.1
  177.4 1.0 copy.71
  (27 shorter events, 4.1 us)
Async XLA Ops:
  8.1 65.9 %copy-start.3 = (f32[2048,128]{1,0:T(8,128)S(1)}, f32[2048,128]{1,0:T(8,128)}, u32[]{:S(2)}) copy-start(f32[2048,128]{1,0:T(8,128)} %param.5) | copy-start | bytes 3145732
  74.5 16.3 %copy-start.1 = (f32[1024,128]{1,0:T(8,128)S(1)}, f32[1024,128]{1,0:T(8,128)}, u32[]{:S(2)}) copy-start(f32[1024,128]{1,0:T(8,128)} %param.4) | copy-start | bytes 1572868
  85.7 7.0 %collective-permute-start = (f32[128,1152]{1,0:T(8,128)}, f32[128,1152]{1,0:T(8,128)S(1)}, u32[]{:S(2)}, u32[]{:S(2)}) collective-permute-start(f32[128,1152]{1,0:T(8,128)} %pad_maximum_fusion.2), channel_id=1, source_target_pairs={{0,1},{1,0},{2,3},{3,2},{4,5},{5,4},{6,7},{7,6},{8,9},{9,8},{10,11... | collective-permute-start | bytes 1769480 | tf_op jit(solution)/shard_map/ppermute | solution.py:47
  157.1 1.0 copy-start.2
  161.3 16.1 %copy-start = (f32[16,128,128]{1,2,0:T(8,128)}, f32[16,128,128]{1,2,0:T(8,128)S(1)}, u32[]{:S(2)}) copy-start(f32[16,128,128]{1,2,0:T(8,128)S(1)} %fusion.18) | copy-start | bytes 3145732
  170.1 6.7 %collective-permute-start.1 = (f32[128,1152]{1,0:T(8,128)S(1)}, f32[128,1152]{1,0:T(8,128)S(1)}, u32[]{:S(2)}, u32[]{:S(2)}) collective-permute-start(f32[128,1152]{1,0:T(8,128)S(1)} %pad_maximum_fusion.3), channel_id=1, source_target_pairs={{0,1},{1,0},{2,3},{3,2},{4,5},{5,4},{6,7},{7,6},{8,9},{9,8},{10,11... | collective-permute-start | bytes 1769480 | tf_op jit(solution)/shard_map/ppermute | solution.py:47

commit v5 on v4

--- a/solution.py
+++ b/solution.py
@@ -29,6 +29,12 @@
 
 
 def all_reduce(x, axes, n):
+    if n & (n - 1) == 0:
+        d = 1
+        while d < n:
+            x = x + lax.ppermute(x, axes, [(j, j ^ d) for j in range(n)])
+            d *= 2
+        return x
     copies = jnp.broadcast_to(x[None], (n, *x.shape))
     return lax.all_to_all(copies, axes, 0, 0, tiled=False).sum(0)
 

time: 179 us -> 169 us (0.944)
  blocking collectives: 120 us -> 75.7 us
  starting transfers between devices: 10.2 us -> 30.7 us
  waiting for transfers between devices: 2.47 us -> 16.9 us
    all_to_all x2 -> x0, blocking collectives: 41.7 us -> none  [all_reduce(): return lax.all_to_all(copies, axes, 0, 0, tiled=False).sum(0)]
    ppermute x0 -> x6, starting transfers between devices: none -> 18.3 us  [all_reduce(): x = x + lax.ppermute(x, axes, [(j, j ^ d) for j in range(n)])]
    ppermute x0 -> x6, waiting for transfers between devices: none -> 14.4 us  [all_reduce(): x = x + lax.ppermute(x, axes, [(j, j ^ d) for j in range(n)])]
    all_to_all x2, blocking collectives: 34.2 us -> 31.5 us  [all_gather(): held = lax.all_to_all(copies, axes, 0, 0, tiled=False)]
    ppermute x2, starting transfers between devices: 10.2 us -> 12.4 us  [samp_sum(): return x + lax.ppermute(x, 'samp', [(0, 1), (1, 0)])]
  transfers between devices with their start and end apart: 2 -> 8, of which waited for: 2 -> 8; matrix products, arithmetic and copies ran while one was open for 1% -> 1% of each run, Pallas kernels for 0% -> 0%
where the time goes in v5:
time: 169 us
  blocking collectives  75.7 us (45%)
  matrix products  35.7 us (21%)
  starting transfers between devices  30.7 us (18%)
  waiting for transfers between devices  16.9 us (10%)
  local copies, waits for them, and re-layouts  5.96 us (4%)
  other arithmetic  2.94 us (2%)
    all_to_all x2, blocking collectives, reduce_scatter(): return lax.all_to_all(chunks, axes, 0, 0, tiled=False).sum(0)  44.3 us
    dot_general x11, matrix products, dot(): jnp.einsum(spec, left, right, precision=HI, preferred_element_type=jnp.fl...  35.1 us
    all_to_all x2, blocking collectives, all_gather(): held = lax.all_to_all(copies, axes, 0, 0, tiled=False)  31.5 us
    ppermute x6, starting transfers between devices, all_reduce(): x = x + lax.ppermute(x, axes, [(j, j ^ d) for j in range(n)])  18.3 us
    ppermute x6, waiting for transfers between devices, all_reduce(): x = x + lax.ppermute(x, axes, [(j, j ^ d) for j in range(n)])  14.4 us
    ppermute x2, starting transfers between devices, samp_sum(): return x + lax.ppermute(x, 'samp', [(0, 1), (1, 0)])  12.4 us
    unnamed x12, local copies, waits for them, and re-layouts  5.63 us
  transfers between devices with their start and end apart: 8, of which 8 were waited for; matrix products, arithmetic and copies ran while one was open for 1% of the time, Pallas kernels for 0%

profile of v5, /device:TPU:1, one launch (start us, length us, event | category | flops | bytes accessed | tf_op | source)
XLA Modules:
  0.0 168.8 jit_solution(13587949708402041017)
XLA Ops:
  0.6 1.8 %convolution_bitcast_fusion.4 = f32[16,8,128]{2,1,0:T(8,128)S(1)} fusion(f32[1024,128]{1,0:T(8,128)} %param.4), kind=kOutput, calls=%fused_computation.21 | convolution fusion | flops 100663296 | bytes 589824 | tf_op jit(solution)/shard_map/ku,lu->kl/dot_general | solution.py:57
  2.5 5.6 %fusion.12 = f32[16,128,128]{2,1,0:T(8,128)S(1)} fusion(f32[1024,128]{1,0:T(8,128)} %param.4, f32[1024,2048]{1,0:T(8,128)} %param.3), kind=kOutput, calls=%fused_computation.12 | convolution fusion | flops 1610612736 | bytes 9961472 | tf_op jit(solution)/shard_map/ku,ujs->jks/dot_general | solution.py:57
  8.2 24.4 %all_to_all.20 = f32[16,136,128]{2,1,0:T(8,128)S(1)} all-to-all(f32[16,136,128]{2,1,0:T(8,128)S(1)} %pad_maximum_fusion), channel_id=1, replica_groups=mesh['uz'=8,'uy'=4,'ux'=4,'samp'=2] {'uy','ux'}, dimensions={0} | all-to-all | bytes 2228224 | tf_op jit(solution)/shard_map/all_to_all | solution.py:22
  32.6 1.7 %collective-permute-start = (f32[136,128]{1,0:T(8,128)S(1)}, f32[136,128]{1,0:T(8,128)S(1)}, u32[]{:S(2)}, u32[]{:S(2)}) collective-permute-start(f32[136,128]{1,0:T(8,128)S(1)} %reduce_sum.18), channel_id=1, source_target_pairs={{0,32},{32,0},{64,96},{96,64},{128,160},{160,128},{192,224},{224,1... | collective-permute-start | bytes 208904 | tf_op jit(solution)/shard_map/ppermute | solution.py:35
  34.4 1.7 %collective-permute-done = f32[136,128]{1,0:T(8,128)S(1)} collective-permute-done((f32[136,128]{1,0:T(8,128)S(1)}, f32[136,128]{1,0:T(8,128)S(1)}, u32[]{:S(2)}, u32[]{:S(2)}) %collective-permute-start) | collective-permute-done | bytes 69664 | tf_op jit(solution)/shard_map/ppermute | solution.py:35
  36.1 3.1 %collective-permute-start.1 = (f32[136,128]{1,0:T(8,128)S(1)}, f32[136,128]{1,0:T(8,128)S(1)}, u32[]{:S(2)}, u32[]{:S(2)}) collective-permute-start(f32[136,128]{1,0:T(8,128)S(1)} %add.24), channel_id=1, source_target_pairs={{0,64},{32,96},{64,0},{96,32},{128,192},{160,224},{192,128},{224,1... | collective-permute-start | bytes 208904 | tf_op jit(solution)/shard_map/ppermute | solution.py:35
  39.2 1.7 %collective-permute-done.1 = f32[136,128]{1,0:T(8,128)S(1)} collective-permute-done((f32[136,128]{1,0:T(8,128)S(1)}, f32[136,128]{1,0:T(8,128)S(1)}, u32[]{:S(2)}, u32[]{:S(2)}) %collective-permute-start.1) | collective-permute-done | bytes 69664 | tf_op jit(solution)/shard_map/ppermute | solution.py:35
  40.9 6.9 %collective-permute-start.2 = (f32[136,128]{1,0:T(8,128)S(1)}, f32[136,128]{1,0:T(8,128)S(1)}, u32[]{:S(2)}, u32[]{:S(2)}) collective-permute-start(f32[136,128]{1,0:T(8,128)S(1)} %add.25), channel_id=1, source_target_pairs={{0,128},{32,160},{64,192},{96,224},{128,0},{160,32},{192,64},{224,... | collective-permute-start | bytes 208904 | tf_op jit(solution)/shard_map/ppermute | solution.py:35
  47.8 2.4 %collective-permute-done.2 = f32[136,128]{1,0:T(8,128)S(1)} collective-permute-done((f32[136,128]{1,0:T(8,128)S(1)}, f32[136,128]{1,0:T(8,128)S(1)}, u32[]{:S(2)}, u32[]{:S(2)}) %collective-permute-start.2) | collective-permute-done | bytes 69664 | tf_op jit(solution)/shard_map/ppermute | solution.py:35
  50.3 15.6 %all_to_all.21 = f32[16,136,128]{2,1,0:T(8,128)S(1)} all-to-all(f32[16,136,128]{2,1,0:T(8,128)S(1)} %broadcast_in_dim.4), channel_id=1, replica_groups=mesh['uz'=8,'uy'=4,'ux'=4,'samp'=2] {'uy','ux'}, dimensions={0} | all-to-all | bytes 2228224 | tf_op jit(solution)/shard_map/all_to_all | solution.py:27
  67.8 1.6 multiply_divide_fusion
  70.4 7.7 %fusion.19 = f32[128,1024]{1,0:T(8,128)S(1)} fusion(f32[16,128,128]{1,2,0:T(8,128)S(1)} %multiply_divide_fusion, f32[1024,2048]{1,0:T(8,128)} %param.3), kind=kOutput, calls=%fused_computation.16 | convolution fusion | flops 1610612736 | bytes 9961472 | tf_op jit(solution)/shard_map/jks,ujs->ku/dot_general | solution.py:57
  79.0 6.2 %collective-permute-start.3 = (f32[128,1152]{1,0:T(8,128)}, f32[128,1152]{1,0:T(8,128)S(1)}, u32[]{:S(2)}, u32[]{:S(2)}) collective-permute-start(f32[128,1152]{1,0:T(8,128)} %pad_maximum_fusion.2), channel_id=1, source_target_pairs={{0,1},{1,0},{2,3},{3,2},{4,5},{5,4},{6,7},{7,6},{8,9},{9,8},{10,11... | collective-permute-start | bytes 1769480 | tf_op jit(solution)/shard_map/ppermute | solution.py:53
  89.0 6.0 %fusion.15 = f32[16,128,128]{2,1,0:T(8,128)S(1)} fusion(f32[128,1024]{1,0:T(8,128)S(1)} %fusion.29, f32[1024,2048]{1,0:T(8,128)} %param.3), kind=kOutput, calls=%fused_computation.13 | convolution fusion | flops 1610612736 | bytes 9961472 | tf_op jit(solution)/shard_map/ku,ujs->jks/dot_general | solution.py:57
  95.2 19.9 %all_to_all.22 = f32[16,136,128]{2,1,0:T(8,128)S(1)} all-to-all(f32[16,136,128]{2,1,0:T(8,128)S(1)} %pad_maximum_fusion.1), channel_id=1, replica_groups=mesh['uz'=8,'uy'=4,'ux'=4,'samp'=2] {'uy','ux'}, dimensions={0} | all-to-all | bytes 2228224 | tf_op jit(solution)/shard_map/all_to_all | solution.py:22
  115.2 3.1 %collective-permute-done.4 = f32[136,128]{1,0:T(8,128)S(1)} collective-permute-done((f32[136,128]{1,0:T(8,128)S(1)}, f32[136,128]{1,0:T(8,128)S(1)}, u32[]{:S(2)}, u32[]{:S(2)}) %collective-permute-start.4) | collective-permute-done | bytes 69664 | tf_op jit(solution)/shard_map/ppermute | solution.py:35
  119.3 3.7 %collective-permute-done.5 = f32[136,128]{1,0:T(8,128)S(1)} collective-permute-done((f32[136,128]{1,0:T(8,128)S(1)}, f32[136,128]{1,0:T(8,128)S(1)}, u32[]{:S(2)}, u32[]{:S(2)}) %collective-permute-start.5) | collective-permute-done | bytes 69664 | tf_op jit(solution)/shard_map/ppermute | solution.py:35
  123.0 5.5 %collective-permute-start.6 = (f32[136,128]{1,0:T(8,128)S(1)}, f32[136,128]{1,0:T(8,128)S(1)}, u32[]{:S(2)}, u32[]{:S(2)}) collective-permute-start(f32[136,128]{1,0:T(8,128)S(1)} %add.29), channel_id=1, source_target_pairs={{0,128},{32,160},{64,192},{96,224},{128,0},{160,32},{192,64},{224,... | collective-permute-start | bytes 208904 | tf_op jit(solution)/shard_map/ppermute | solution.py:35
  128.5 1.8 %collective-permute-done.6 = f32[136,128]{1,0:T(8,128)S(1)} collective-permute-done((f32[136,128]{1,0:T(8,128)S(1)}, f32[136,128]{1,0:T(8,128)S(1)}, u32[]{:S(2)}, u32[]{:S(2)}) %collective-permute-start.6) | collective-permute-done | bytes 69664 | tf_op jit(solution)/shard_map/ppermute | solution.py:35
  130.4 15.9 %all_to_all.23 = f32[16,136,128]{2,1,0:T(8,128)S(1)} all-to-all(f32[16,136,128]{2,1,0:T(8,128)S(1)} %broadcast_in_dim.5), channel_id=1, replica_groups=mesh['uz'=8,'uy'=4,'ux'=4,'samp'=2] {'uy','ux'}, dimensions={0} | all-to-all | bytes 2228224 | tf_op jit(solution)/shard_map/all_to_all | solution.py:27
  148.7 1.8 %fusion.18 = f32[16,128,128]{1,2,0:T(8,128)S(1)} fusion(f32[16,128,128]{1,2,0:T(8,128)S(1)} %multiply_divide_fusion, f32[16,128,128]{1,2,0:T(8,128)} %copy.68, f32[16,136,128]{2,1,0:T(8,128)} %copy-done.2), kind=kOutput, calls=%fused_computation.15 | convolution fusion | flops 201850880 | bytes 4259840 | tf_op jit(solution)/shard_map/kl,jks->jls/dot_general | solution.py:57
  151.6 7.7 %fusion.22 = f32[128,1024]{1,0:T(8,128)S(1)} fusion(f32[16,128,128]{1,2,0:T(8,128)S(1)} %fusion.18, f32[1024,2048]{1,0:T(8,128)} %param.3), kind=kOutput, calls=%fused_computation.17 | convolution fusion | flops 1610612736 | bytes 9961472 | tf_op jit(solution)/shard_map/jks,ujs->ku/dot_general | solution.py:57
  159.4 6.2 %collective-permute-start.7 = (f32[128,1152]{1,0:T(8,128)S(1)}, f32[128,1152]{1,0:T(8,128)S(1)}, u32[]{:S(2)}, u32[]{:S(2)}) collective-permute-start(f32[128,1152]{1,0:T(8,128)S(1)} %pad_maximum_fusion.3), channel_id=1, source_target_pairs={{0,1},{1,0},{2,3},{3,2},{4,5},{5,4},{6,7},{7,6},{8,9},{9,8},{10,11... | collective-permute-start | bytes 1769480 | tf_op jit(solution)/shard_map/ppermute | solution.py:53
  165.6 1.6 collective-permute-done.7
  (39 shorter events, 14.1 us)
Async XLA Ops:
  8.1 59.2 %copy-start.3 = (f32[2048,128]{1,0:T(8,128)S(1)}, f32[2048,128]{1,0:T(8,128)}, u32[]{:S(2)}) copy-start(f32[2048,128]{1,0:T(8,128)} %param.5) | copy-start | bytes 3145732
  32.6 3.4 %collective-permute-start = (f32[136,128]{1,0:T(8,128)S(1)}, f32[136,128]{1,0:T(8,128)S(1)}, u32[]{:S(2)}, u32[]{:S(2)}) collective-permute-start(f32[136,128]{1,0:T(8,128)S(1)} %reduce_sum.18), channel_id=1, source_target_pairs={{0,32},{32,0},{64,96},{96,64},{128,160},{160,128},{192,224},{224,1... | collective-permute-start | bytes 208904 | tf_op jit(solution)/shard_map/ppermute | solution.py:35
  36.1 4.8 %collective-permute-start.1 = (f32[136,128]{1,0:T(8,128)S(1)}, f32[136,128]{1,0:T(8,128)S(1)}, u32[]{:S(2)}, u32[]{:S(2)}) collective-permute-start(f32[136,128]{1,0:T(8,128)S(1)} %add.24), channel_id=1, source_target_pairs={{0,64},{32,96},{64,0},{96,32},{128,192},{160,224},{192,128},{224,1... | collective-permute-start | bytes 208904 | tf_op jit(solution)/shard_map/ppermute | solution.py:35
  40.9 9.3 %collective-permute-start.2 = (f32[136,128]{1,0:T(8,128)S(1)}, f32[136,128]{1,0:T(8,128)S(1)}, u32[]{:S(2)}, u32[]{:S(2)}) collective-permute-start(f32[136,128]{1,0:T(8,128)S(1)} %add.25), channel_id=1, source_target_pairs={{0,128},{32,160},{64,192},{96,224},{128,0},{160,32},{192,64},{224,... | collective-permute-start | bytes 208904 | tf_op jit(solution)/shard_map/ppermute | solution.py:35
  67.8 17.4 %copy-start.1 = (f32[1024,128]{1,0:T(8,128)S(1)}, f32[1024,128]{1,0:T(8,128)}, u32[]{:S(2)}) copy-start(f32[1024,128]{1,0:T(8,128)} %param.4) | copy-start | bytes 1572868
  79.0 8.1 %collective-permute-start.3 = (f32[128,1152]{1,0:T(8,128)}, f32[128,1152]{1,0:T(8,128)S(1)}, u32[]{:S(2)}, u32[]{:S(2)}) collective-permute-start(f32[128,1152]{1,0:T(8,128)} %pad_maximum_fusion.2), channel_id=1, source_target_pairs={{0,1},{1,0},{2,3},{3,2},{4,5},{5,4},{6,7},{7,6},{8,9},{9,8},{10,11... | collective-permute-start | bytes 1769480 | tf_op jit(solution)/shard_map/ppermute | solution.py:53
  115.1 3.2 %collective-permute-start.4 = (f32[136,128]{1,0:T(8,128)S(1)}, f32[136,128]{1,0:T(8,128)S(1)}, u32[]{:S(2)}, u32[]{:S(2)}) collective-permute-start(f32[136,128]{1,0:T(8,128)S(1)} %reduce_sum.19), channel_id=1, source_target_pairs={{0,32},{32,0},{64,96},{96,64},{128,160},{160,128},{192,224},{224,1... | collective-permute-start | bytes 208904 | tf_op jit(solution)/shard_map/ppermute | solution.py:35
  118.4 4.6 %collective-permute-start.5 = (f32[136,128]{1,0:T(8,128)S(1)}, f32[136,128]{1,0:T(8,128)S(1)}, u32[]{:S(2)}, u32[]{:S(2)}) collective-permute-start(f32[136,128]{1,0:T(8,128)S(1)} %add.28), channel_id=1, source_target_pairs={{0,64},{32,96},{64,0},{96,32},{128,192},{160,224},{192,128},{224,1... | collective-permute-start | bytes 208904 | tf_op jit(solution)/shard_map/ppermute | solution.py:35
  123.0 7.3 %collective-permute-start.6 = (f32[136,128]{1,0:T(8,128)S(1)}, f32[136,128]{1,0:T(8,128)S(1)}, u32[]{:S(2)}, u32[]{:S(2)}) collective-permute-start(f32[136,128]{1,0:T(8,128)S(1)} %add.29), channel_id=1, source_target_pairs={{0,128},{32,160},{64,192},{96,224},{128,0},{160,32},{192,64},{224,... | collective-permute-start | bytes 208904 | tf_op jit(solution)/shard_map/ppermute | solution.py:35
  146.3 1.0 copy-start.2
  150.6 17.2 %copy-start = (f32[16,128,128]{1,2,0:T(8,128)}, f32[16,128,128]{1,2,0:T(8,128)S(1)}, u32[]{:S(2)}) copy-start(f32[16,128,128]{1,2,0:T(8,128)S(1)} %fusion.18) | copy-start | bytes 3145732
  159.4 7.8 %collective-permute-start.7 = (f32[128,1152]{1,0:T(8,128)S(1)}, f32[128,1152]{1,0:T(8,128)S(1)}, u32[]{:S(2)}, u32[]{:S(2)}) collective-permute-start(f32[128,1152]{1,0:T(8,128)S(1)} %pad_maximum_fusion.3), channel_id=1, source_target_pairs={{0,1},{1,0},{2,3},{3,2},{4,5},{5,4},{6,7},{7,6},{8,9},{9,8},{10,11... | collective-permute-start | bytes 1769480 | tf_op jit(solution)/shard_map/ppermute | solution.py:53

commit v6 on v4

--- a/solution.py
+++ b/solution.py
@@ -29,6 +29,20 @@
 
 
 def all_reduce(x, axes, n):
+    if n % 2 == 0 and n >= 4:
+        x = x + lax.ppermute(x, axes, [(j, j ^ 1) for j in range(n)])
+        groups = n // 2
+        mine = lax.axis_index(axes) // 2
+        got = [x] + [
+            lax.ppermute(x, axes, [(j, (((j // 2) ^ t) * 2) + j % 2) for j in range(n)])
+            for t in range(1, groups)
+        ]
+        held = jnp.stack(got)
+        ordered = jnp.take(held, jnp.arange(groups) ^ mine, axis=0)
+        total = ordered[0]
+        for g in range(1, groups):
+            total = total + ordered[g]
+        return total
     copies = jnp.broadcast_to(x[None], (n, *x.shape))
     return lax.all_to_all(copies, axes, 0, 0, tiled=False).sum(0)
 

time: 179 us -> 173 us (0.966)
  blocking collectives: 120 us -> 59.6 us
  waiting for transfers between devices: 2.47 us -> 34.4 us
  starting transfers between devices: 10.2 us -> 31 us
    all_to_all x2 -> x0, blocking collectives: 41.7 us -> none  [all_reduce(): return lax.all_to_all(copies, axes, 0, 0, tiled=False).sum(0)]
    all_to_all x2 -> x1, blocking collectives: 44.3 us -> 19.9 us  [reduce_scatter(): return lax.all_to_all(chunks, axes, 0, 0, tiled=False).sum(0)]
    all_to_all x0 -> x1, waiting for transfers between devices: none -> 16.7 us  [reduce_scatter(): return lax.all_to_all(chunks, axes, 0, 0, tiled=False).sum(0)]
    ppermute x0 -> x8, starting transfers between devices: none -> 15.7 us  [the longest x6 13.9 us: all_reduce(): lax.ppermute(x, axes, [(j, (j // 2 ^ t) * 2 + j % 2) for j in range(n)])]
    ppermute x0 -> x8, waiting for transfers between devices: none -> 15.3 us  [the longest x6 10.5 us: all_reduce(): lax.ppermute(x, axes, [(j, (j // 2 ^ t) * 2 + j % 2) for j in range(n)])]
    all_to_all x0 -> x1, starting transfers between devices: none -> 7.58 us  [reduce_scatter(): return lax.all_to_all(chunks, axes, 0, 0, tiled=False).sum(0)]
    all_to_all x2, blocking collectives: 34.2 us -> 39.7 us  [all_gather(): held = lax.all_to_all(copies, axes, 0, 0, tiled=False)]
    ppermute x2, starting transfers between devices: 10.2 us -> 7.76 us  [samp_sum(): return x + lax.ppermute(x, 'samp', [(0, 1), (1, 0)])]
  transfers between devices with their start and end apart: 2 -> 11, of which waited for: 2 -> 7; matrix products, arithmetic and copies ran while one was open for 1% -> 1% of each run, Pallas kernels for 0% -> 0%
where the time goes in v6:
time: 173 us
  blocking collectives  59.6 us (34%)
  matrix products  35.7 us (21%)
  waiting for transfers between devices  34.4 us (20%)
  starting transfers between devices  31 us (18%)
  local copies, waits for them, and re-layouts  7.09 us (4%)
  other arithmetic  4.16 us (2%)
    all_to_all x2, blocking collectives, all_gather(): held = lax.all_to_all(copies, axes, 0, 0, tiled=False)  39.7 us
    dot_general x11, matrix products, dot(): jnp.einsum(spec, left, right, precision=HI, preferred_element_type=jnp.fl...  35.1 us
    all_to_all x1, blocking collectives, reduce_scatter(): return lax.all_to_all(chunks, axes, 0, 0, tiled=False).sum(0)  19.9 us
    all_to_all x1, waiting for transfers between devices, reduce_scatter(): return lax.all_to_all(chunks, axes, 0, 0, tiled=False).sum(0)  16.7 us
    ppermute x6, starting transfers between devices, all_reduce(): lax.ppermute(x, axes, [(j, (j // 2 ^ t) * 2 + j % 2) for j in range(n)])  13.9 us
    ppermute x6, waiting for transfers between devices, all_reduce(): lax.ppermute(x, axes, [(j, (j // 2 ^ t) * 2 + j % 2) for j in range(n)])  10.5 us
    ppermute x2, starting transfers between devices, samp_sum(): return x + lax.ppermute(x, 'samp', [(0, 1), (1, 0)])  7.76 us
    all_to_all x1, starting transfers between devices, reduce_scatter(): return lax.all_to_all(chunks, axes, 0, 0, tiled=False).sum(0)  7.58 us
  transfers between devices with their start and end apart: 11, of which 7 were waited for; matrix products, arithmetic and copies ran while one was open for 1% of the time, Pallas kernels for 0%

profile of v6, /device:TPU:1, one launch (start us, length us, event | category | flops | bytes accessed | tf_op | source)
XLA Modules:
  0.0 172.9 jit_solution(4173164466735612085)
XLA Ops:
  0.6 1.8 %convolution_bitcast_fusion.4 = f32[16,8,128]{2,1,0:T(8,128)S(1)} fusion(f32[1024,128]{1,0:T(8,128)} %param.6), kind=kOutput, calls=%fused_computation.23 | convolution fusion | flops 100663296 | bytes 589824 | tf_op jit(solution)/shard_map/ku,lu->kl/dot_general | solution.py:65
  2.5 5.6 %fusion.12 = f32[16,128,128]{2,1,0:T(8,128)S(1)} fusion(f32[1024,128]{1,0:T(8,128)} %param.6, f32[1024,2048]{1,0:T(8,128)} %param.5), kind=kOutput, calls=%fused_computation.14 | convolution fusion | flops 1610612736 | bytes 9961472 | tf_op jit(solution)/shard_map/ku,ujs->jks/dot_general | solution.py:65
  9.2 7.6 %all-to-all-start = ((f32[16,136,128]{2,1,0:T(8,128)}), f32[16,136,128]{2,1,0:T(8,128)S(1)}, u32[]{:S(2)}, u32[]{:S(2)}) async-start(f32[16,136,128]{2,1,0:T(8,128)} %pad_maximum_fusion), calls=%async_computation | async-start | bytes 2228224 | tf_op jit(solution)/shard_map/all_to_all | solution.py:22
  16.8 16.7 %all-to-all-done = f32[16,136,128]{2,1,0:T(8,128)S(1)} async-done(((f32[16,136,128]{2,1,0:T(8,128)}), f32[16,136,128]{2,1,0:T(8,128)S(1)}, u32[]{:S(2)}, u32[]{:S(2)}) %all-to-all-start) | async-done | bytes 1114144 | tf_op jit(solution)/shard_map/all_to_all | solution.py:22
  33.5 1.7 collective-permute-start
  35.3 1.7 collective-permute-done
  37.0 5.9 %collective-permute-start.3 = (f32[136,128]{1,0:T(8,128)S(1)}, f32[136,128]{1,0:T(8,128)S(1)}, u32[]{:S(2)}, u32[]{:S(2)}) collective-permute-start(f32[136,128]{1,0:T(8,128)S(1)} %add.40), channel_id=1, source_target_pairs={{0,192},{32,224},{64,128},{96,160},{128,64},{160,96},{192,0},{224,... | collective-permute-start | bytes 208904 | tf_op jit(solution)/shard_map/ppermute | solution.py:37
  45.1 5.5 %collective-permute-done.2 = f32[136,128]{1,0:T(8,128)S(1)} collective-permute-done((f32[136,128]{1,0:T(8,128)S(1)}, f32[136,128]{1,0:T(8,128)S(1)}, u32[]{:S(2)}, u32[]{:S(2)}) %collective-permute-start.2) | collective-permute-done | bytes 69664 | tf_op jit(solution)/shard_map/ppermute | solution.py:37
  51.4 22.3 %all_to_all.20 = f32[16,136,128]{2,1,0:T(8,128)S(1)} all-to-all(f32[16,136,128]{2,1,0:T(8,128)S(1)} %broadcast_in_dim.26), channel_id=1, replica_groups=mesh['uz'=8,'uy'=4,'ux'=4,'samp'=2] {'uy','ux'}, dimensions={0} | all-to-all | bytes 2228224 | tf_op jit(solution)/shard_map/all_to_all | solution.py:27
  75.7 1.6 multiply_divide_fusion
  78.3 7.7 %fusion.19 = f32[128,1024]{1,0:T(8,128)S(1)} fusion(f32[16,128,128]{1,2,0:T(8,128)S(1)} %multiply_divide_fusion, f32[1024,2048]{1,0:T(8,128)} %param.5), kind=kOutput, calls=%fused_computation.18 | convolution fusion | flops 1610612736 | bytes 9961472 | tf_op jit(solution)/shard_map/jks,ujs->ku/dot_general | solution.py:65
  86.9 2.8 %collective-permute-start.4 = (f32[128,1152]{1,0:T(8,128)}, f32[128,1152]{1,0:T(8,128)S(1)}, u32[]{:S(2)}, u32[]{:S(2)}) collective-permute-start(f32[128,1152]{1,0:T(8,128)} %pad_maximum_fusion.2), channel_id=1, source_target_pairs={{0,1},{1,0},{2,3},{3,2},{4,5},{5,4},{6,7},{7,6},{8,9},{9,8},{10,11... | collective-permute-start | bytes 1769480 | tf_op jit(solution)/shard_map/ppermute | solution.py:61
  91.6 1.5 fusion.29
  93.5 6.0 %fusion.15 = f32[16,128,128]{2,1,0:T(8,128)S(1)} fusion(f32[128,1024]{1,0:T(8,128)S(1)} %fusion.29, f32[1024,2048]{1,0:T(8,128)} %param.5), kind=kOutput, calls=%fused_computation.15 | convolution fusion | flops 1610612736 | bytes 9961472 | tf_op jit(solution)/shard_map/ku,ujs->jks/dot_general | solution.py:65
  99.6 19.9 %all_to_all.21 = f32[16,136,128]{2,1,0:T(8,128)S(1)} all-to-all(f32[16,136,128]{2,1,0:T(8,128)S(1)} %pad_maximum_fusion.1), channel_id=1, replica_groups=mesh['uz'=8,'uy'=4,'ux'=4,'samp'=2] {'uy','ux'}, dimensions={0} | all-to-all | bytes 2228224 | tf_op jit(solution)/shard_map/all_to_all | solution.py:22
  119.7 3.1 %collective-permute-done.5 = f32[136,128]{1,0:T(8,128)S(1)} collective-permute-done((f32[136,128]{1,0:T(8,128)S(1)}, f32[136,128]{1,0:T(8,128)S(1)}, u32[]{:S(2)}, u32[]{:S(2)}) %collective-permute-start.5) | collective-permute-done | bytes 69664 | tf_op jit(solution)/shard_map/ppermute | solution.py:33
  122.8 2.8 %collective-permute-start.8 = (f32[136,128]{1,0:T(8,128)S(1)}, f32[136,128]{1,0:T(8,128)S(1)}, u32[]{:S(2)}, u32[]{:S(2)}) collective-permute-start(f32[136,128]{1,0:T(8,128)S(1)} %add.45), channel_id=1, source_target_pairs={{0,192},{32,224},{64,128},{96,160},{128,64},{160,96},{192,0},{224,... | collective-permute-start | bytes 208904 | tf_op jit(solution)/shard_map/ppermute | solution.py:37
  125.6 1.9 %collective-permute-start.7 = (f32[136,128]{1,0:T(8,128)S(1)}, f32[136,128]{1,0:T(8,128)S(1)}, u32[]{:S(2)}, u32[]{:S(2)}) collective-permute-start(f32[136,128]{1,0:T(8,128)S(1)} %add.45), channel_id=1, source_target_pairs={{0,128},{32,160},{64,192},{96,224},{128,0},{160,32},{192,64},{224,... | collective-permute-start | bytes 208904 | tf_op jit(solution)/shard_map/ppermute | solution.py:37
  128.6 4.9 %collective-permute-done.7 = f32[136,128]{1,0:T(8,128)S(1)} collective-permute-done((f32[136,128]{1,0:T(8,128)S(1)}, f32[136,128]{1,0:T(8,128)S(1)}, u32[]{:S(2)}, u32[]{:S(2)}) %collective-permute-start.7) | collective-permute-done | bytes 69664 | tf_op jit(solution)/shard_map/ppermute | solution.py:37
  134.3 17.4 %all_to_all.22 = f32[16,136,128]{2,1,0:T(8,128)S(1)} all-to-all(f32[16,136,128]{2,1,0:T(8,128)S(1)} %broadcast_in_dim.28), channel_id=1, replica_groups=mesh['uz'=8,'uy'=4,'ux'=4,'samp'=2] {'uy','ux'}, dimensions={0} | all-to-all | bytes 2228224 | tf_op jit(solution)/shard_map/all_to_all | solution.py:27
  154.1 1.8 %fusion.18 = f32[16,128,128]{1,2,0:T(8,128)S(1)} fusion(f32[16,128,128]{1,2,0:T(8,128)S(1)} %multiply_divide_fusion, f32[16,128,128]{1,2,0:T(8,128)} %copy.70, f32[16,136,128]{2,1,0:T(8,128)} %copy-done.2), kind=kOutput, calls=%fused_computation.17 | convolution fusion | flops 201850880 | bytes 4259840 | tf_op jit(solution)/shard_map/kl,jks->jls/dot_general | solution.py:65
  156.9 7.7 %fusion.22 = f32[128,1024]{1,0:T(8,128)S(1)} fusion(f32[16,128,128]{1,2,0:T(8,128)S(1)} %fusion.18, f32[1024,2048]{1,0:T(8,128)} %param.5), kind=kOutput, calls=%fused_computation.19 | convolution fusion | flops 1610612736 | bytes 9961472 | tf_op jit(solution)/shard_map/jks,ujs->ku/dot_general | solution.py:65
  164.7 5.0 %collective-permute-start.9 = (f32[128,1152]{1,0:T(8,128)S(1)}, f32[128,1152]{1,0:T(8,128)S(1)}, u32[]{:S(2)}, u32[]{:S(2)}) collective-permute-start(f32[128,1152]{1,0:T(8,128)S(1)} %pad_maximum_fusion.3), channel_id=1, source_target_pairs={{0,1},{1,0},{2,3},{3,2},{4,5},{5,4},{6,7},{7,6},{8,9},{9,8},{10,11... | collective-permute-start | bytes 1769480 | tf_op jit(solution)/shard_map/ppermute | solution.py:61
  169.7 1.6 collective-permute-done.9
  (51 shorter events, 17.3 us)
Async XLA Ops:
  8.1 67.1 %copy-start.3 = (f32[2048,128]{1,0:T(8,128)S(1)}, f32[2048,128]{1,0:T(8,128)}, u32[]{:S(2)}) copy-start(f32[2048,128]{1,0:T(8,128)} %param.7) | copy-start | bytes 3145732
  9.2 24.3 %all-to-all-start = ((f32[16,136,128]{2,1,0:T(8,128)}), f32[16,136,128]{2,1,0:T(8,128)S(1)}, u32[]{:S(2)}, u32[]{:S(2)}) async-start(f32[16,136,128]{2,1,0:T(8,128)} %pad_maximum_fusion), calls=%async_computation | async-start | bytes 2228224 | tf_op jit(solution)/shard_map/all_to_all | solution.py:22
  33.5 3.4 %collective-permute-start = (f32[136,128]{1,0:T(8,128)S(1)}, f32[136,128]{1,0:T(8,128)S(1)}, u32[]{:S(2)}, u32[]{:S(2)}) collective-permute-start(f32[136,128]{1,0:T(8,128)S(1)} %reduce_sum.18), channel_id=1, source_target_pairs={{0,32},{32,0},{64,96},{96,64},{128,160},{160,128},{192,224},{224,1... | collective-permute-start | bytes 208904 | tf_op jit(solution)/shard_map/ppermute | solution.py:33
  37.0 8.1 %collective-permute-start.3 = (f32[136,128]{1,0:T(8,128)S(1)}, f32[136,128]{1,0:T(8,128)S(1)}, u32[]{:S(2)}, u32[]{:S(2)}) collective-permute-start(f32[136,128]{1,0:T(8,128)S(1)} %add.40), channel_id=1, source_target_pairs={{0,192},{32,224},{64,128},{96,160},{128,64},{160,96},{192,0},{224,... | collective-permute-start | bytes 208904 | tf_op jit(solution)/shard_map/ppermute | solution.py:37
  42.9 7.7 %collective-permute-start.2 = (f32[136,128]{1,0:T(8,128)S(1)}, f32[136,128]{1,0:T(8,128)S(1)}, u32[]{:S(2)}, u32[]{:S(2)}) collective-permute-start(f32[136,128]{1,0:T(8,128)S(1)} %add.40), channel_id=1, source_target_pairs={{0,128},{32,160},{64,192},{96,224},{128,0},{160,32},{192,64},{224,... | collective-permute-start | bytes 208904 | tf_op jit(solution)/shard_map/ppermute | solution.py:37
  43.9 6.8 %collective-permute-start.1 = (f32[136,128]{1,0:T(8,128)S(1)}, f32[136,128]{1,0:T(8,128)S(1)}, u32[]{:S(2)}, u32[]{:S(2)}) collective-permute-start(f32[136,128]{1,0:T(8,128)S(1)} %add.40), channel_id=1, source_target_pairs={{0,64},{32,96},{64,0},{96,32},{128,192},{160,224},{192,128},{224,1... | collective-permute-start | bytes 208904 | tf_op jit(solution)/shard_map/ppermute | solution.py:37
  75.7 14.0 %copy-start.1 = (f32[1024,128]{1,0:T(8,128)S(1)}, f32[1024,128]{1,0:T(8,128)}, u32[]{:S(2)}) copy-start(f32[1024,128]{1,0:T(8,128)} %param.6) | copy-start | bytes 1572868
  86.9 4.6 %collective-permute-start.4 = (f32[128,1152]{1,0:T(8,128)}, f32[128,1152]{1,0:T(8,128)S(1)}, u32[]{:S(2)}, u32[]{:S(2)}) collective-permute-start(f32[128,1152]{1,0:T(8,128)} %pad_maximum_fusion.2), channel_id=1, source_target_pairs={{0,1},{1,0},{2,3},{3,2},{4,5},{5,4},{6,7},{7,6},{8,9},{9,8},{10,11... | collective-permute-start | bytes 1769480 | tf_op jit(solution)/shard_map/ppermute | solution.py:61
  119.6 3.2 %collective-permute-start.5 = (f32[136,128]{1,0:T(8,128)S(1)}, f32[136,128]{1,0:T(8,128)S(1)}, u32[]{:S(2)}, u32[]{:S(2)}) collective-permute-start(f32[136,128]{1,0:T(8,128)S(1)} %reduce_sum.19), channel_id=1, source_target_pairs={{0,32},{32,0},{64,96},{96,64},{128,160},{160,128},{192,224},{224,1... | collective-permute-start | bytes 208904 | tf_op jit(solution)/shard_map/ppermute | solution.py:33
  122.8 5.7 %collective-permute-start.8 = (f32[136,128]{1,0:T(8,128)S(1)}, f32[136,128]{1,0:T(8,128)S(1)}, u32[]{:S(2)}, u32[]{:S(2)}) collective-permute-start(f32[136,128]{1,0:T(8,128)S(1)} %add.45), channel_id=1, source_target_pairs={{0,192},{32,224},{64,128},{96,160},{128,64},{160,96},{192,0},{224,... | collective-permute-start | bytes 208904 | tf_op jit(solution)/shard_map/ppermute | solution.py:37
  125.6 7.9 %collective-permute-start.7 = (f32[136,128]{1,0:T(8,128)S(1)}, f32[136,128]{1,0:T(8,128)S(1)}, u32[]{:S(2)}, u32[]{:S(2)}) collective-permute-start(f32[136,128]{1,0:T(8,128)S(1)} %add.45), channel_id=1, source_target_pairs={{0,128},{32,160},{64,192},{96,224},{128,0},{160,32},{192,64},{224,... | collective-permute-start | bytes 208904 | tf_op jit(solution)/shard_map/ppermute | solution.py:37
  127.5 6.0 %collective-permute-start.6 = (f32[136,128]{1,0:T(8,128)S(1)}, f32[136,128]{1,0:T(8,128)S(1)}, u32[]{:S(2)}, u32[]{:S(2)}) collective-permute-start(f32[136,128]{1,0:T(8,128)S(1)} %add.45), channel_id=1, source_target_pairs={{0,64},{32,96},{64,0},{96,32},{128,192},{160,224},{192,128},{224,1... | collective-permute-start | bytes 208904 | tf_op jit(solution)/shard_map/ppermute | solution.py:37
  151.7 1.0 copy-start.2
  155.9 15.9 %copy-start = (f32[16,128,128]{1,2,0:T(8,128)}, f32[16,128,128]{1,2,0:T(8,128)S(1)}, u32[]{:S(2)}) copy-start(f32[16,128,128]{1,2,0:T(8,128)S(1)} %fusion.18) | copy-start | bytes 3145732
  164.7 6.6 %collective-permute-start.9 = (f32[128,1152]{1,0:T(8,128)S(1)}, f32[128,1152]{1,0:T(8,128)S(1)}, u32[]{:S(2)}, u32[]{:S(2)}) collective-permute-start(f32[128,1152]{1,0:T(8,128)S(1)} %pad_maximum_fusion.3), channel_id=1, source_target_pairs={{0,1},{1,0},{2,3},{3,2},{4,5},{5,4},{6,7},{7,6},{8,9},{9,8},{10,11... | collective-permute-start | bytes 1769480 | tf_op jit(solution)/shard_map/ppermute | solution.py:61

commit v7 on v5

--- a/solution.py
+++ b/solution.py
@@ -30,10 +30,10 @@
 
 def all_reduce(x, axes, n):
     if n & (n - 1) == 0:
-        d = 1
-        while d < n:
+        d = n // 2
+        while d >= 1:
             x = x + lax.ppermute(x, axes, [(j, j ^ d) for j in range(n)])
-            d *= 2
+            d //= 2
         return x
     copies = jnp.broadcast_to(x[None], (n, *x.shape))
     return lax.all_to_all(copies, axes, 0, 0, tiled=False).sum(0)

time: 169 us -> 170 us (level)
  starting transfers between devices: 30.7 us -> 26.3 us
  waiting for transfers between devices: 16.9 us -> 19.5 us
  blocking collectives: 75.7 us -> 77.9 us
    ppermute x6, waiting for transfers between devices: 14.4 us -> 17 us  [all_reduce(): x = x + lax.ppermute(x, axes, [(j, j ^ d) for j in range(n)])]
    ppermute x2, starting transfers between devices: 12.4 us -> 9.97 us  [samp_sum(): return x + lax.ppermute(x, 'samp', [(0, 1), (1, 0)])]
    all_to_all x2, blocking collectives: 31.5 us -> 33.6 us  [all_gather(): held = lax.all_to_all(copies, axes, 0, 0, tiled=False)]
    ppermute x6, starting transfers between devices: 18.3 us -> 16.4 us  [all_reduce(): x = x + lax.ppermute(x, axes, [(j, j ^ d) for j in range(n)])]
where the time goes in v7:
time: 170 us; the launch traced here: 169 us
  blocking collectives  77.9 us (46%)
  matrix products  35.7 us (21%)
  starting transfers between devices  26.3 us (15%)
  waiting for transfers between devices  19.5 us (11%)
  local copies, waits for them, and re-layouts  5.96 us (4%)
  other arithmetic  2.94 us (2%)
    all_to_all x2, blocking collectives, reduce_scatter(): return lax.all_to_all(chunks, axes, 0, 0, tiled=False).sum(0)  44.3 us
    dot_general x11, matrix products, dot(): jnp.einsum(spec, left, right, precision=HI, preferred_element_type=jnp.fl...  35.1 us
    all_to_all x2, blocking collectives, all_gather(): held = lax.all_to_all(copies, axes, 0, 0, tiled=False)  33.6 us
    ppermute x6, waiting for transfers between devices, all_reduce(): x = x + lax.ppermute(x, axes, [(j, j ^ d) for j in range(n)])  17 us
    ppermute x6, starting transfers between devices, all_reduce(): x = x + lax.ppermute(x, axes, [(j, j ^ d) for j in range(n)])  16.4 us
    ppermute x2, starting transfers between devices, samp_sum(): return x + lax.ppermute(x, 'samp', [(0, 1), (1, 0)])  9.97 us
    unnamed x12, local copies, waits for them, and re-layouts  5.63 us
  transfers between devices with their start and end apart: 8, of which 8 were waited for; matrix products, arithmetic and copies ran while one was open for 1% of the time, Pallas kernels for 0%

profile of v7, /device:TPU:1, one launch (start us, length us, event | category | flops | bytes accessed | tf_op | source)
XLA Modules:
  0.0 169.2 jit_solution(12014360693961027645)
XLA Ops:
  0.6 1.8 %convolution_bitcast_fusion.4 = f32[16,8,128]{2,1,0:T(8,128)S(1)} fusion(f32[1024,128]{1,0:T(8,128)} %param.4), kind=kOutput, calls=%fused_computation.21 | convolution fusion | flops 100663296 | bytes 589824 | tf_op jit(solution)/shard_map/ku,lu->kl/dot_general | solution.py:57
  2.5 5.6 %fusion.12 = f32[16,128,128]{2,1,0:T(8,128)S(1)} fusion(f32[1024,128]{1,0:T(8,128)} %param.4, f32[1024,2048]{1,0:T(8,128)} %param.3), kind=kOutput, calls=%fused_computation.12 | convolution fusion | flops 1610612736 | bytes 9961472 | tf_op jit(solution)/shard_map/ku,ujs->jks/dot_general | solution.py:57
  8.2 24.4 %all_to_all.20 = f32[16,136,128]{2,1,0:T(8,128)S(1)} all-to-all(f32[16,136,128]{2,1,0:T(8,128)S(1)} %pad_maximum_fusion), channel_id=1, replica_groups=mesh['uz'=8,'uy'=4,'ux'=4,'samp'=2] {'uy','ux'}, dimensions={0} | all-to-all | bytes 2228224 | tf_op jit(solution)/shard_map/all_to_all | solution.py:22
  32.6 7.0 %collective-permute-start = (f32[136,128]{1,0:T(8,128)S(1)}, f32[136,128]{1,0:T(8,128)S(1)}, u32[]{:S(2)}, u32[]{:S(2)}) collective-permute-start(f32[136,128]{1,0:T(8,128)S(1)} %reduce_sum.18), channel_id=1, source_target_pairs={{0,128},{32,160},{64,192},{96,224},{128,0},{160,32},{192,64},{224,... | collective-permute-start | bytes 208904 | tf_op jit(solution)/shard_map/ppermute | solution.py:35
  39.6 1.8 %collective-permute-done = f32[136,128]{1,0:T(8,128)S(1)} collective-permute-done((f32[136,128]{1,0:T(8,128)S(1)}, f32[136,128]{1,0:T(8,128)S(1)}, u32[]{:S(2)}, u32[]{:S(2)}) %collective-permute-start) | collective-permute-done | bytes 69664 | tf_op jit(solution)/shard_map/ppermute | solution.py:35
  41.5 2.2 %collective-permute-start.1 = (f32[136,128]{1,0:T(8,128)S(1)}, f32[136,128]{1,0:T(8,128)S(1)}, u32[]{:S(2)}, u32[]{:S(2)}) collective-permute-start(f32[136,128]{1,0:T(8,128)S(1)} %add.24), channel_id=1, source_target_pairs={{0,64},{32,96},{64,0},{96,32},{128,192},{160,224},{192,128},{224,1... | collective-permute-start | bytes 208904 | tf_op jit(solution)/shard_map/ppermute | solution.py:35
  43.6 3.2 %collective-permute-done.1 = f32[136,128]{1,0:T(8,128)S(1)} collective-permute-done((f32[136,128]{1,0:T(8,128)S(1)}, f32[136,128]{1,0:T(8,128)S(1)}, u32[]{:S(2)}, u32[]{:S(2)}) %collective-permute-start.1) | collective-permute-done | bytes 69664 | tf_op jit(solution)/shard_map/ppermute | solution.py:35
  47.0 3.1 %collective-permute-done.2 = f32[136,128]{1,0:T(8,128)S(1)} collective-permute-done((f32[136,128]{1,0:T(8,128)S(1)}, f32[136,128]{1,0:T(8,128)S(1)}, u32[]{:S(2)}, u32[]{:S(2)}) %collective-permute-start.2) | collective-permute-done | bytes 69664 | tf_op jit(solution)/shard_map/ppermute | solution.py:35
  50.2 16.9 %all_to_all.21 = f32[16,136,128]{2,1,0:T(8,128)S(1)} all-to-all(f32[16,136,128]{2,1,0:T(8,128)S(1)} %broadcast_in_dim.4), channel_id=1, replica_groups=mesh['uz'=8,'uy'=4,'ux'=4,'samp'=2] {'uy','ux'}, dimensions={0} | all-to-all | bytes 2228224 | tf_op jit(solution)/shard_map/all_to_all | solution.py:27
  69.1 1.6 multiply_divide_fusion
  71.7 7.7 %fusion.19 = f32[128,1024]{1,0:T(8,128)S(1)} fusion(f32[16,128,128]{1,2,0:T(8,128)S(1)} %multiply_divide_fusion, f32[1024,2048]{1,0:T(8,128)} %param.3), kind=kOutput, calls=%fused_computation.16 | convolution fusion | flops 1610612736 | bytes 9961472 | tf_op jit(solution)/shard_map/jks,ujs->ku/dot_general | solution.py:57
  80.3 4.9 %collective-permute-start.3 = (f32[128,1152]{1,0:T(8,128)}, f32[128,1152]{1,0:T(8,128)S(1)}, u32[]{:S(2)}, u32[]{:S(2)}) collective-permute-start(f32[128,1152]{1,0:T(8,128)} %pad_maximum_fusion.2), channel_id=1, source_target_pairs={{0,1},{1,0},{2,3},{3,2},{4,5},{5,4},{6,7},{7,6},{8,9},{9,8},{10,11... | collective-permute-start | bytes 1769480 | tf_op jit(solution)/shard_map/ppermute | solution.py:53
  87.0 1.5 fusion.29
  88.9 6.0 %fusion.15 = f32[16,128,128]{2,1,0:T(8,128)S(1)} fusion(f32[128,1024]{1,0:T(8,128)S(1)} %fusion.29, f32[1024,2048]{1,0:T(8,128)} %param.3), kind=kOutput, calls=%fused_computation.13 | convolution fusion | flops 1610612736 | bytes 9961472 | tf_op jit(solution)/shard_map/ku,ujs->jks/dot_general | solution.py:57
  95.1 19.9 %all_to_all.22 = f32[16,136,128]{2,1,0:T(8,128)S(1)} all-to-all(f32[16,136,128]{2,1,0:T(8,128)S(1)} %pad_maximum_fusion.1), channel_id=1, replica_groups=mesh['uz'=8,'uy'=4,'ux'=4,'samp'=2] {'uy','ux'}, dimensions={0} | all-to-all | bytes 2228224 | tf_op jit(solution)/shard_map/all_to_all | solution.py:22
  115.0 5.7 %collective-permute-start.4 = (f32[136,128]{1,0:T(8,128)S(1)}, f32[136,128]{1,0:T(8,128)S(1)}, u32[]{:S(2)}, u32[]{:S(2)}) collective-permute-start(f32[136,128]{1,0:T(8,128)S(1)} %reduce_sum.19), channel_id=1, source_target_pairs={{0,128},{32,160},{64,192},{96,224},{128,0},{160,32},{192,64},{224,... | collective-permute-start | bytes 208904 | tf_op jit(solution)/shard_map/ppermute | solution.py:35
  120.7 1.7 %collective-permute-done.4 = f32[136,128]{1,0:T(8,128)S(1)} collective-permute-done((f32[136,128]{1,0:T(8,128)S(1)}, f32[136,128]{1,0:T(8,128)S(1)}, u32[]{:S(2)}, u32[]{:S(2)}) %collective-permute-start.4) | collective-permute-done | bytes 69664 | tf_op jit(solution)/shard_map/ppermute | solution.py:35
  123.8 4.0 %collective-permute-done.5 = f32[136,128]{1,0:T(8,128)S(1)} collective-permute-done((f32[136,128]{1,0:T(8,128)S(1)}, f32[136,128]{1,0:T(8,128)S(1)}, u32[]{:S(2)}, u32[]{:S(2)}) %collective-permute-start.5) | collective-permute-done | bytes 69664 | tf_op jit(solution)/shard_map/ppermute | solution.py:35
  127.9 3.1 %collective-permute-done.6 = f32[136,128]{1,0:T(8,128)S(1)} collective-permute-done((f32[136,128]{1,0:T(8,128)S(1)}, f32[136,128]{1,0:T(8,128)S(1)}, u32[]{:S(2)}, u32[]{:S(2)}) %collective-permute-start.6) | collective-permute-done | bytes 69664 | tf_op jit(solution)/shard_map/ppermute | solution.py:35
  131.1 16.8 %all_to_all.23 = f32[16,136,128]{2,1,0:T(8,128)S(1)} all-to-all(f32[16,136,128]{2,1,0:T(8,128)S(1)} %broadcast_in_dim.5), channel_id=1, replica_groups=mesh['uz'=8,'uy'=4,'ux'=4,'samp'=2] {'uy','ux'}, dimensions={0} | all-to-all | bytes 2228224 | tf_op jit(solution)/shard_map/all_to_all | solution.py:27
  150.3 1.8 %fusion.18 = f32[16,128,128]{1,2,0:T(8,128)S(1)} fusion(f32[16,128,128]{1,2,0:T(8,128)S(1)} %multiply_divide_fusion, f32[16,128,128]{1,2,0:T(8,128)} %copy.68, f32[16,136,128]{2,1,0:T(8,128)} %copy-done.2), kind=kOutput, calls=%fused_computation.15 | convolution fusion | flops 201850880 | bytes 4259840 | tf_op jit(solution)/shard_map/kl,jks->jls/dot_general | solution.py:57
  153.1 7.7 %fusion.22 = f32[128,1024]{1,0:T(8,128)S(1)} fusion(f32[16,128,128]{1,2,0:T(8,128)S(1)} %fusion.18, f32[1024,2048]{1,0:T(8,128)} %param.3), kind=kOutput, calls=%fused_computation.17 | convolution fusion | flops 1610612736 | bytes 9961472 | tf_op jit(solution)/shard_map/jks,ujs->ku/dot_general | solution.py:57
  160.9 5.1 %collective-permute-start.7 = (f32[128,1152]{1,0:T(8,128)S(1)}, f32[128,1152]{1,0:T(8,128)S(1)}, u32[]{:S(2)}, u32[]{:S(2)}) collective-permute-start(f32[128,1152]{1,0:T(8,128)S(1)} %pad_maximum_fusion.3), channel_id=1, source_target_pairs={{0,1},{1,0},{2,3},{3,2},{4,5},{5,4},{6,7},{7,6},{8,9},{9,8},{10,11... | collective-permute-start | bytes 1769480 | tf_op jit(solution)/shard_map/ppermute | solution.py:53
  166.0 1.6 collective-permute-done.7
  (39 shorter events, 13.1 us)
Async XLA Ops:
  8.1 60.4 %copy-start.3 = (f32[2048,128]{1,0:T(8,128)S(1)}, f32[2048,128]{1,0:T(8,128)}, u32[]{:S(2)}) copy-start(f32[2048,128]{1,0:T(8,128)} %param.5) | copy-start | bytes 3145732
  32.6 8.8 %collective-permute-start = (f32[136,128]{1,0:T(8,128)S(1)}, f32[136,128]{1,0:T(8,128)S(1)}, u32[]{:S(2)}, u32[]{:S(2)}) collective-permute-start(f32[136,128]{1,0:T(8,128)S(1)} %reduce_sum.18), channel_id=1, source_target_pairs={{0,128},{32,160},{64,192},{96,224},{128,0},{160,32},{192,64},{224,... | collective-permute-start | bytes 208904 | tf_op jit(solution)/shard_map/ppermute | solution.py:35
  41.5 5.4 %collective-permute-start.1 = (f32[136,128]{1,0:T(8,128)S(1)}, f32[136,128]{1,0:T(8,128)S(1)}, u32[]{:S(2)}, u32[]{:S(2)}) collective-permute-start(f32[136,128]{1,0:T(8,128)S(1)} %add.24), channel_id=1, source_target_pairs={{0,64},{32,96},{64,0},{96,32},{128,192},{160,224},{192,128},{224,1... | collective-permute-start | bytes 208904 | tf_op jit(solution)/shard_map/ppermute | solution.py:35
  46.9 3.2 %collective-permute-start.2 = (f32[136,128]{1,0:T(8,128)S(1)}, f32[136,128]{1,0:T(8,128)S(1)}, u32[]{:S(2)}, u32[]{:S(2)}) collective-permute-start(f32[136,128]{1,0:T(8,128)S(1)} %add.25), channel_id=1, source_target_pairs={{0,32},{32,0},{64,96},{96,64},{128,160},{160,128},{192,224},{224,1... | collective-permute-start | bytes 208904 | tf_op jit(solution)/shard_map/ppermute | solution.py:35
  69.1 16.0 %copy-start.1 = (f32[1024,128]{1,0:T(8,128)S(1)}, f32[1024,128]{1,0:T(8,128)}, u32[]{:S(2)}) copy-start(f32[1024,128]{1,0:T(8,128)} %param.4) | copy-start | bytes 1572868
  80.3 6.7 %collective-permute-start.3 = (f32[128,1152]{1,0:T(8,128)}, f32[128,1152]{1,0:T(8,128)S(1)}, u32[]{:S(2)}, u32[]{:S(2)}) collective-permute-start(f32[128,1152]{1,0:T(8,128)} %pad_maximum_fusion.2), channel_id=1, source_target_pairs={{0,1},{1,0},{2,3},{3,2},{4,5},{5,4},{6,7},{7,6},{8,9},{9,8},{10,11... | collective-permute-start | bytes 1769480 | tf_op jit(solution)/shard_map/ppermute | solution.py:53
  115.0 7.4 %collective-permute-start.4 = (f32[136,128]{1,0:T(8,128)S(1)}, f32[136,128]{1,0:T(8,128)S(1)}, u32[]{:S(2)}, u32[]{:S(2)}) collective-permute-start(f32[136,128]{1,0:T(8,128)S(1)} %reduce_sum.19), channel_id=1, source_target_pairs={{0,128},{32,160},{64,192},{96,224},{128,0},{160,32},{192,64},{224,... | collective-permute-start | bytes 208904 | tf_op jit(solution)/shard_map/ppermute | solution.py:35
  122.5 5.3 %collective-permute-start.5 = (f32[136,128]{1,0:T(8,128)S(1)}, f32[136,128]{1,0:T(8,128)S(1)}, u32[]{:S(2)}, u32[]{:S(2)}) collective-permute-start(f32[136,128]{1,0:T(8,128)S(1)} %add.28), channel_id=1, source_target_pairs={{0,64},{32,96},{64,0},{96,32},{128,192},{160,224},{192,128},{224,1... | collective-permute-start | bytes 208904 | tf_op jit(solution)/shard_map/ppermute | solution.py:35
  127.8 3.2 %collective-permute-start.6 = (f32[136,128]{1,0:T(8,128)S(1)}, f32[136,128]{1,0:T(8,128)S(1)}, u32[]{:S(2)}, u32[]{:S(2)}) collective-permute-start(f32[136,128]{1,0:T(8,128)S(1)} %add.29), channel_id=1, source_target_pairs={{0,32},{32,0},{64,96},{96,64},{128,160},{160,128},{192,224},{224,1... | collective-permute-start | bytes 208904 | tf_op jit(solution)/shard_map/ppermute | solution.py:35
  147.9 1.0 copy-start.2
  152.1 16.1 %copy-start = (f32[16,128,128]{1,2,0:T(8,128)}, f32[16,128,128]{1,2,0:T(8,128)S(1)}, u32[]{:S(2)}) copy-start(f32[16,128,128]{1,2,0:T(8,128)S(1)} %fusion.18) | copy-start | bytes 3145732
  160.9 6.7 %collective-permute-start.7 = (f32[128,1152]{1,0:T(8,128)S(1)}, f32[128,1152]{1,0:T(8,128)S(1)}, u32[]{:S(2)}, u32[]{:S(2)}) collective-permute-start(f32[128,1152]{1,0:T(8,128)S(1)} %pad_maximum_fusion.3), channel_id=1, source_target_pairs={{0,1},{1,0},{2,3},{3,2},{4,5},{5,4},{6,7},{7,6},{8,9},{9,8},{10,11... | collective-permute-start | bytes 1769480 | tf_op jit(solution)/shard_map/ppermute | solution.py:53

commit v8 on v5

--- a/solution.py
+++ b/solution.py
@@ -39,11 +39,11 @@
     return lax.all_to_all(copies, axes, 0, 0, tiled=False).sum(0)
 
 
-def unit_sum(x, stages):
+def unit_sum(x, stages, own=lambda piece: piece):
     *outer, (last, n_last) = stages
     for axes, n in outer:
         x = reduce_scatter(x, axes, n)
-    x = all_reduce(x, last, n_last)
+    x = own(all_reduce(x, last, n_last))
     for axes, n in reversed(outer):
         x = all_gather(x, axes, n)
     return x
@@ -68,8 +68,14 @@
         target_h = dot("ku,ujs->jks", unitig, wide)
         width = rows // n
         both = jnp.concatenate([target_h, gram_unit.reshape(n, -1, width)], axis=1)
-        both = unit_sum(both.reshape(-1, width), stages).reshape(n, -1, width)
-        target_h, gram_unit = both[:, :k], both[:, k:].reshape(k, k)
+        if width == k:
+            turn = lambda piece: jnp.concatenate([piece[:k].T, piece[k:]])
+            both = unit_sum(both.reshape(-1, width), stages, turn).reshape(n, -1, width)
+            target_h = both[:, :k].transpose(0, 2, 1)
+        else:
+            both = unit_sum(both.reshape(-1, width), stages).reshape(n, -1, width)
+            target_h = both[:, :k]
+        gram_unit = both[:, k:].reshape(k, k)
         sample = sample * target_h / dot("kl,jks->jls", gram_unit, sample)
         gram_sample = dot("jks,jls->kl", sample, sample)
         both = samp_sum(jnp.concatenate([dot("jks,ujs->ku", sample, wide), gram_sample], axis=1))

time: 169 us -> 169 us (level)
  other arithmetic: 2.94 us -> 5.46 us
  waiting for transfers between devices: 16.9 us -> 14.6 us
    ppermute x2, waiting for transfers between devices: 2.47 us -> 0.23 us  [samp_sum(): return x + lax.ppermute(x, 'samp', [(0, 1), (1, 0)])]
    unnamed x12 -> x14, local copies, waits for them, and re-layouts: 5.63 us -> 5.22 us
  transfers between devices with their start and end apart: 8 -> 8, of which waited for: 8 -> 7; matrix products, arithmetic and copies ran while one was open for 1% -> 2% of each run, Pallas kernels for 0% -> 0%
where the time goes in v8:
time: 169 us
  blocking collectives  77 us (46%)
  matrix products  34.9 us (21%)
  starting transfers between devices  30.2 us (18%)
  waiting for transfers between devices  14.6 us (9%)
  local copies, waits for them, and re-layouts  5.56 us (3%)
  other arithmetic  5.46 us (3%)
    all_to_all x2, blocking collectives, reduce_scatter(): return lax.all_to_all(chunks, axes, 0, 0, tiled=False).sum(0)  45.3 us
    dot_general x11, matrix products, dot(): jnp.einsum(spec, left, right, precision=HI, preferred_element_type=jnp.fl...  34.4 us
    all_to_all x2, blocking collectives, all_gather(): held = lax.all_to_all(copies, axes, 0, 0, tiled=False)  31.7 us
    ppermute x6, starting transfers between devices, all_reduce(): x = x + lax.ppermute(x, axes, [(j, j ^ d) for j in range(n)])  18.3 us
    ppermute x6, waiting for transfers between devices, all_reduce(): x = x + lax.ppermute(x, axes, [(j, j ^ d) for j in range(n)])  14.4 us
    ppermute x2, starting transfers between devices, samp_sum(): return x + lax.ppermute(x, 'samp', [(0, 1), (1, 0)])  12 us
    unnamed x14, local copies, waits for them, and re-layouts  5.22 us
  transfers between devices with their start and end apart: 8, of which 7 were waited for; matrix products, arithmetic and copies ran while one was open for 2% of the time, Pallas kernels for 0%

profile of v8, /device:TPU:1, one launch (start us, length us, event | category | flops | bytes accessed | tf_op | source)
XLA Modules:
  0.0 168.7 jit_solution(617280968323183576)
XLA Ops:
  0.6 1.8 %convolution_bitcast_fusion.3 = f32[16,8,128]{2,1,0:T(8,128)S(1)} fusion(f32[1024,128]{1,0:T(8,128)} %param.4), kind=kOutput, calls=%fused_computation.19 | convolution fusion | flops 100663296 | bytes 589824 | tf_op jit(solution)/shard_map/ku,lu->kl/dot_general | solution.py:57
  2.5 5.7 %fusion.12 = f32[16,128,128]{2,1,0:T(8,128)S(1)} fusion(f32[1024,128]{1,0:T(8,128)} %param.4, f32[1024,2048]{1,0:T(8,128)} %param.3), kind=kOutput, calls=%fused_computation.12 | convolution fusion | flops 1610612736 | bytes 9961472 | tf_op jit(solution)/shard_map/ku,ujs->jks/dot_general | solution.py:57
  8.3 24.3 %all_to_all.20 = f32[16,136,128]{2,1,0:T(8,128)S(1)} all-to-all(f32[16,136,128]{2,1,0:T(8,128)S(1)} %pad_maximum_fusion), channel_id=1, replica_groups=mesh['uz'=8,'uy'=4,'ux'=4,'samp'=2] {'uy','ux'}, dimensions={0} | all-to-all | bytes 2228224 | tf_op jit(solution)/shard_map/all_to_all | solution.py:22
  32.6 1.7 %collective-permute-start = (f32[136,128]{1,0:T(8,128)S(1)}, f32[136,128]{1,0:T(8,128)S(1)}, u32[]{:S(2)}, u32[]{:S(2)}) collective-permute-start(f32[136,128]{1,0:T(8,128)S(1)} %reduce_sum.18), channel_id=1, source_target_pairs={{0,32},{32,0},{64,96},{96,64},{128,160},{160,128},{192,224},{224,1... | collective-permute-start | bytes 208904 | tf_op jit(solution)/shard_map/ppermute | solution.py:35
  34.3 1.7 %collective-permute-done = f32[136,128]{1,0:T(8,128)S(1)} collective-permute-done((f32[136,128]{1,0:T(8,128)S(1)}, f32[136,128]{1,0:T(8,128)S(1)}, u32[]{:S(2)}, u32[]{:S(2)}) %collective-permute-start) | collective-permute-done | bytes 69664 | tf_op jit(solution)/shard_map/ppermute | solution.py:35
  36.0 3.1 %collective-permute-start.1 = (f32[136,128]{1,0:T(8,128)S(1)}, f32[136,128]{1,0:T(8,128)S(1)}, u32[]{:S(2)}, u32[]{:S(2)}) collective-permute-start(f32[136,128]{1,0:T(8,128)S(1)} %add.24), channel_id=1, source_target_pairs={{0,64},{32,96},{64,0},{96,32},{128,192},{160,224},{192,128},{224,1... | collective-permute-start | bytes 208904 | tf_op jit(solution)/shard_map/ppermute | solution.py:35
  39.1 1.7 %collective-permute-done.1 = f32[136,128]{1,0:T(8,128)S(1)} collective-permute-done((f32[136,128]{1,0:T(8,128)S(1)}, f32[136,128]{1,0:T(8,128)S(1)}, u32[]{:S(2)}, u32[]{:S(2)}) %collective-permute-start.1) | collective-permute-done | bytes 69664 | tf_op jit(solution)/shard_map/ppermute | solution.py:35
  40.8 6.9 %collective-permute-start.2 = (f32[136,128]{1,0:T(8,128)S(1)}, f32[136,128]{1,0:T(8,128)S(1)}, u32[]{:S(2)}, u32[]{:S(2)}) collective-permute-start(f32[136,128]{1,0:T(8,128)S(1)} %add.25), channel_id=1, source_target_pairs={{0,128},{32,160},{64,192},{96,224},{128,0},{160,32},{192,64},{224,... | collective-permute-start | bytes 208904 | tf_op jit(solution)/shard_map/ppermute | solution.py:35
  47.8 2.4 %collective-permute-done.2 = f32[136,128]{1,0:T(8,128)S(1)} collective-permute-done((f32[136,128]{1,0:T(8,128)S(1)}, f32[136,128]{1,0:T(8,128)S(1)}, u32[]{:S(2)}, u32[]{:S(2)}) %collective-permute-start.2) | collective-permute-done | bytes 69664 | tf_op jit(solution)/shard_map/ppermute | solution.py:35
  50.4 15.5 %all_to_all.21 = f32[16,136,128]{2,1,0:T(8,128)S(1)} all-to-all(f32[16,136,128]{2,1,0:T(8,128)S(1)} %broadcast_in_dim.4), channel_id=1, replica_groups=mesh['uz'=8,'uy'=4,'ux'=4,'samp'=2] {'uy','ux'}, dimensions={0} | all-to-all | bytes 2228224 | tf_op jit(solution)/shard_map/all_to_all | solution.py:27
  68.7 7.7 %fusion.18 = f32[128,1024]{1,0:T(8,128)S(1)} fusion(f32[16,128,128]{1,2,0:T(8,128)S(1)} %fusion.26, f32[1024,2048]{1,0:T(8,128)} %param.3), kind=kOutput, calls=%fused_computation.14 | convolution fusion | flops 1610612736 | bytes 9961472 | tf_op jit(solution)/shard_map/jks,ujs->ku/dot_general | solution.py:57
  78.1 6.2 %collective-permute-start.3 = (f32[128,1152]{1,0:T(8,128)}, f32[128,1152]{1,0:T(8,128)}, u32[]{:S(2)}, u32[]{:S(2)}) collective-permute-start(f32[128,1152]{1,0:T(8,128)} %pad_maximum_fusion.2), channel_id=1, source_target_pairs={{0,1},{1,0},{2,3},{3,2},{4,5},{5,4},{6,7},{7,6},{8,9},{9,8},{10,11... | collective-permute-start | bytes 1769480 | tf_op jit(solution)/shard_map/ppermute | solution.py:53
  84.3 2.1 %copy.5 = f32[1024,128]{0,1:T(8,128)} copy(f32[1024,128]{1,0:T(8,128)} %param.4) | data formatting | bytes 1048576 | tf_op args[1]
  87.7 1.6 fusion.29
  90.1 6.0 %fusion.15 = f32[16,128,128]{2,1,0:T(8,128)S(1)} fusion(f32[128,1024]{1,0:T(8,128)S(1)} %fusion.29, f32[1024,2048]{1,0:T(8,128)} %param.3), kind=kOutput, calls=%fused_computation.13 | convolution fusion | flops 1610612736 | bytes 9961472 | tf_op jit(solution)/shard_map/ku,ujs->jks/dot_general | solution.py:57
  96.3 21.0 %all_to_all.22 = f32[16,136,128]{2,1,0:T(8,128)} all-to-all(f32[16,136,128]{2,1,0:T(8,128)S(1)} %pad_maximum_fusion.1), channel_id=1, replica_groups=mesh['uz'=8,'uy'=4,'ux'=4,'samp'=2] {'uy','ux'}, dimensions={0} | all-to-all | bytes 2228224 | tf_op jit(solution)/shard_map/all_to_all | solution.py:22
  118.7 3.1 %collective-permute-done.4 = f32[136,128]{1,0:T(8,128)S(1)} collective-permute-done((f32[136,128]{1,0:T(8,128)S(1)}, f32[136,128]{1,0:T(8,128)S(1)}, u32[]{:S(2)}, u32[]{:S(2)}) %collective-permute-start.4) | collective-permute-done | bytes 69664 | tf_op jit(solution)/shard_map/ppermute | solution.py:35
  122.8 3.7 %collective-permute-done.5 = f32[136,128]{1,0:T(8,128)S(1)} collective-permute-done((f32[136,128]{1,0:T(8,128)S(1)}, f32[136,128]{1,0:T(8,128)S(1)}, u32[]{:S(2)}, u32[]{:S(2)}) %collective-permute-start.5) | collective-permute-done | bytes 69664 | tf_op jit(solution)/shard_map/ppermute | solution.py:35
  126.4 5.5 %collective-permute-start.6 = (f32[136,128]{1,0:T(8,128)S(1)}, f32[136,128]{1,0:T(8,128)S(1)}, u32[]{:S(2)}, u32[]{:S(2)}) collective-permute-start(f32[136,128]{1,0:T(8,128)S(1)} %add.29), channel_id=1, source_target_pairs={{0,128},{32,160},{64,192},{96,224},{128,0},{160,32},{192,64},{224,... | collective-permute-start | bytes 208904 | tf_op jit(solution)/shard_map/ppermute | solution.py:35
  131.9 1.8 %collective-permute-done.6 = f32[136,128]{1,0:T(8,128)S(1)} collective-permute-done((f32[136,128]{1,0:T(8,128)S(1)}, f32[136,128]{1,0:T(8,128)S(1)}, u32[]{:S(2)}, u32[]{:S(2)}) %collective-permute-start.6) | collective-permute-done | bytes 69664 | tf_op jit(solution)/shard_map/ppermute | solution.py:35
  134.0 16.2 %all_to_all.23 = f32[16,136,128]{2,1,0:T(8,128)S(1)} all-to-all(f32[16,136,128]{2,1,0:T(8,128)S(1)} %broadcast_in_dim.5), channel_id=1, replica_groups=mesh['uz'=8,'uy'=4,'ux'=4,'samp'=2] {'uy','ux'}, dimensions={0} | all-to-all | bytes 2228224 | tf_op jit(solution)/shard_map/all_to_all | solution.py:27
  151.8 8.0 %fusion.21 = f32[128,1024]{1,0:T(8,128)S(1)} fusion(f32[16,128,128]{1,2,0:T(8,128)S(1)} %get-tuple-element.4, f32[1024,2048]{1,0:T(8,128)} %param.3), kind=kOutput, calls=%fused_computation.15 | convolution fusion | flops 1610612736 | bytes 9961472 | tf_op jit(solution)/shard_map/jks,ujs->ku/dot_general | solution.py:57
  159.8 5.7 %collective-permute-start.7 = (f32[128,1152]{1,0:T(8,128)S(1)}, f32[128,1152]{1,0:T(8,128)S(1)}, u32[]{:S(2)}, u32[]{:S(2)}) collective-permute-start(f32[128,1152]{1,0:T(8,128)S(1)} %pad_maximum_fusion.3), channel_id=1, source_target_pairs={{0,1},{1,0},{2,3},{3,2},{4,5},{5,4},{6,7},{7,6},{8,9},{9,8},{10,11... | collective-permute-start | bytes 1769480 | tf_op jit(solution)/shard_map/ppermute | solution.py:53
  165.6 1.4 multiply_divide_fusion
  (48 shorter events, 12.9 us)
Async XLA Ops:
  2.5 63.5 %copy-start = (f32[2048,128]{1,0:T(8,128)S(1)}, f32[2048,128]{1,0:T(8,128)}, u32[]{:S(2)}) copy-start(f32[2048,128]{1,0:T(8,128)} %param.5) | copy-start | bytes 3145732
  32.6 3.4 %collective-permute-start = (f32[136,128]{1,0:T(8,128)S(1)}, f32[136,128]{1,0:T(8,128)S(1)}, u32[]{:S(2)}, u32[]{:S(2)}) collective-permute-start(f32[136,128]{1,0:T(8,128)S(1)} %reduce_sum.18), channel_id=1, source_target_pairs={{0,32},{32,0},{64,96},{96,64},{128,160},{160,128},{192,224},{224,1... | collective-permute-start | bytes 208904 | tf_op jit(solution)/shard_map/ppermute | solution.py:35
  36.0 4.8 %collective-permute-start.1 = (f32[136,128]{1,0:T(8,128)S(1)}, f32[136,128]{1,0:T(8,128)S(1)}, u32[]{:S(2)}, u32[]{:S(2)}) collective-permute-start(f32[136,128]{1,0:T(8,128)S(1)} %add.24), channel_id=1, source_target_pairs={{0,64},{32,96},{64,0},{96,32},{128,192},{160,224},{192,128},{224,1... | collective-permute-start | bytes 208904 | tf_op jit(solution)/shard_map/ppermute | solution.py:35
  40.8 9.3 %collective-permute-start.2 = (f32[136,128]{1,0:T(8,128)S(1)}, f32[136,128]{1,0:T(8,128)S(1)}, u32[]{:S(2)}, u32[]{:S(2)}) collective-permute-start(f32[136,128]{1,0:T(8,128)S(1)} %add.25), channel_id=1, source_target_pairs={{0,128},{32,160},{64,192},{96,224},{128,0},{160,32},{192,64},{224,... | collective-permute-start | bytes 208904 | tf_op jit(solution)/shard_map/ppermute | solution.py:35
  66.5 1.0 copy-start.1
  76.5 0.8 copy-start.3
  78.1 8.3 %collective-permute-start.3 = (f32[128,1152]{1,0:T(8,128)}, f32[128,1152]{1,0:T(8,128)}, u32[]{:S(2)}, u32[]{:S(2)}) collective-permute-start(f32[128,1152]{1,0:T(8,128)} %pad_maximum_fusion.2), channel_id=1, source_target_pairs={{0,1},{1,0},{2,3},{3,2},{4,5},{5,4},{6,7},{7,6},{8,9},{9,8},{10,11... | collective-permute-start | bytes 1769480 | tf_op jit(solution)/shard_map/ppermute | solution.py:53
  89.3 0.8 copy-start.4
  118.6 3.2 %collective-permute-start.4 = (f32[136,128]{1,0:T(8,128)S(1)}, f32[136,128]{1,0:T(8,128)S(1)}, u32[]{:S(2)}, u32[]{:S(2)}) collective-permute-start(f32[136,128]{1,0:T(8,128)S(1)} %reduce_sum.19), channel_id=1, source_target_pairs={{0,32},{32,0},{64,96},{96,64},{128,160},{160,128},{192,224},{224,1... | collective-permute-start | bytes 208904 | tf_op jit(solution)/shard_map/ppermute | solution.py:35
  121.8 4.6 %collective-permute-start.5 = (f32[136,128]{1,0:T(8,128)S(1)}, f32[136,128]{1,0:T(8,128)S(1)}, u32[]{:S(2)}, u32[]{:S(2)}) collective-permute-start(f32[136,128]{1,0:T(8,128)S(1)} %add.28), channel_id=1, source_target_pairs={{0,64},{32,96},{64,0},{96,32},{128,192},{160,224},{192,128},{224,1... | collective-permute-start | bytes 208904 | tf_op jit(solution)/shard_map/ppermute | solution.py:35
  126.4 7.3 %collective-permute-start.6 = (f32[136,128]{1,0:T(8,128)S(1)}, f32[136,128]{1,0:T(8,128)S(1)}, u32[]{:S(2)}, u32[]{:S(2)}) collective-permute-start(f32[136,128]{1,0:T(8,128)S(1)} %add.29), channel_id=1, source_target_pairs={{0,128},{32,160},{64,192},{96,224},{128,0},{160,32},{192,64},{224,... | collective-permute-start | bytes 208904 | tf_op jit(solution)/shard_map/ppermute | solution.py:35
  150.2 15.4 %copy-start.2 = (f32[128,2048]{0,1:S(1)}, f32[128,2048]{0,1}, u32[]{:S(2)}) copy-start(f32[128,2048]{0,1} %copy-done.1) | copy-start | bytes 3145732
  151.8 15.5 %copy-start.5 = (f32[128,1024]{1,0:T(8,128)S(1)}, f32[128,1024]{1,0:T(8,128)}, u32[]{:S(2)}) copy-start(f32[128,1024]{1,0:T(8,128)} %copy-done.4) | copy-start | bytes 1572868
  159.8 7.4 %collective-permute-start.7 = (f32[128,1152]{1,0:T(8,128)S(1)}, f32[128,1152]{1,0:T(8,128)S(1)}, u32[]{:S(2)}, u32[]{:S(2)}) collective-permute-start(f32[128,1152]{1,0:T(8,128)S(1)} %pad_maximum_fusion.3), channel_id=1, source_target_pairs={{0,1},{1,0},{2,3},{3,2},{4,5},{5,4},{6,7},{7,6},{8,9},{9,8},{10,11... | collective-permute-start | bytes 1769480 | tf_op jit(solution)/shard_map/ppermute | solution.py:53

commit v9 on v8

--- a/solution.py
+++ b/solution.py
@@ -61,7 +61,7 @@
     n = stages[0][1]
     rows, k = sample_factor.shape
     wide = abundance.reshape(abundance.shape[0], n, rows // n)
-    unitig = unitig_factor.T
+    unitig = lax.optimization_barrier(unitig_factor.T)
     sample = sample_factor.reshape(n, rows // n, k).transpose(0, 2, 1)
     for sweep in range(ITERS):
         gram_unit = dot("ku,lu->kl", unitig, unitig)

time: 169 us -> 162 us (0.959)
  matrix products: 34.9 us -> 29.9 us
  other arithmetic: 5.46 us -> 3.45 us
  local copies, waits for them, and re-layouts: 5.56 us -> 3.59 us
  waiting for transfers between devices: 14.6 us -> 16.3 us
    dot_general x11, matrix products: 34.4 us -> 29.3 us  [dot(): jnp.einsum(spec, left, right, precision=HI, preferred_element_type=jnp.fl...]
    unnamed x14 -> x20, local copies, waits for them, and re-layouts: 5.22 us -> 3.25 us
  transfers between devices with their start and end apart: 8 -> 8, of which waited for: 7 -> 8; matrix products, arithmetic and copies ran while one was open for 2% -> 1% of each run, Pallas kernels for 0% -> 0%
where the time goes in v9:
time: 162 us
  blocking collectives  76.9 us (47%)
  starting transfers between devices  30.5 us (19%)
  matrix products  29.9 us (18%)
  waiting for transfers between devices  16.3 us (10%)
  local copies, waits for them, and re-layouts  3.59 us (2%)
  other arithmetic  3.45 us (2%)
    all_to_all x2, blocking collectives, reduce_scatter(): return lax.all_to_all(chunks, axes, 0, 0, tiled=False).sum(0)  45.2 us
    all_to_all x2, blocking collectives, all_gather(): held = lax.all_to_all(copies, axes, 0, 0, tiled=False)  31.7 us
    dot_general x11, matrix products, dot(): jnp.einsum(spec, left, right, precision=HI, preferred_element_type=jnp.fl...  29.3 us
    ppermute x6, starting transfers between devices, all_reduce(): x = x + lax.ppermute(x, axes, [(j, j ^ d) for j in range(n)])  18.3 us
    ppermute x6, waiting for transfers between devices, all_reduce(): x = x + lax.ppermute(x, axes, [(j, j ^ d) for j in range(n)])  14.4 us
    ppermute x2, starting transfers between devices, samp_sum(): return x + lax.ppermute(x, 'samp', [(0, 1), (1, 0)])  12.2 us
    unnamed x20, local copies, waits for them, and re-layouts  3.25 us
  transfers between devices with their start and end apart: 8, of which 8 were waited for; matrix products, arithmetic and copies ran while one was open for 1% of the time, Pallas kernels for 0%

profile of v9, /device:TPU:1, one launch (start us, length us, event | category | flops | bytes accessed | tf_op | source)
XLA Modules:
  0.0 161.6 jit_solution(11498876039961329621)
XLA Ops:
  0.6 1.2 copy.5
  2.3 5.6 %fusion.12 = f32[16,128,128]{2,1,0:T(8,128)S(1)} fusion(f32[128,1024]{1,0:T(8,128)S(1)} %bitcast.114, f32[1024,2048]{1,0:T(8,128)} %param.3), kind=kOutput, calls=%fused_computation.12 | convolution fusion | flops 1610612736 | bytes 9961472 | tf_op jit(solution)/shard_map/ku,ujs->jks/dot_general | solution.py:57
  8.0 24.3 %all_to_all.20 = f32[16,136,128]{2,1,0:T(8,128)S(1)} all-to-all(f32[16,136,128]{2,1,0:T(8,128)S(1)} %pad_maximum_fusion), channel_id=1, replica_groups=mesh['uz'=8,'uy'=4,'ux'=4,'samp'=2] {'uy','ux'}, dimensions={0} | all-to-all | bytes 2228224 | tf_op jit(solution)/shard_map/all_to_all | solution.py:22
  32.4 1.7 %collective-permute-start = (f32[136,128]{1,0:T(8,128)S(1)}, f32[136,128]{1,0:T(8,128)S(1)}, u32[]{:S(2)}, u32[]{:S(2)}) collective-permute-start(f32[136,128]{1,0:T(8,128)S(1)} %reduce_sum.18), channel_id=1, source_target_pairs={{0,32},{32,0},{64,96},{96,64},{128,160},{160,128},{192,224},{224,1... | collective-permute-start | bytes 208904 | tf_op jit(solution)/shard_map/ppermute | solution.py:35
  34.1 1.7 %collective-permute-done = f32[136,128]{1,0:T(8,128)S(1)} collective-permute-done((f32[136,128]{1,0:T(8,128)S(1)}, f32[136,128]{1,0:T(8,128)S(1)}, u32[]{:S(2)}, u32[]{:S(2)}) %collective-permute-start) | collective-permute-done | bytes 69664 | tf_op jit(solution)/shard_map/ppermute | solution.py:35
  35.8 3.1 %collective-permute-start.1 = (f32[136,128]{1,0:T(8,128)S(1)}, f32[136,128]{1,0:T(8,128)S(1)}, u32[]{:S(2)}, u32[]{:S(2)}) collective-permute-start(f32[136,128]{1,0:T(8,128)S(1)} %add.24), channel_id=1, source_target_pairs={{0,64},{32,96},{64,0},{96,32},{128,192},{160,224},{192,128},{224,1... | collective-permute-start | bytes 208904 | tf_op jit(solution)/shard_map/ppermute | solution.py:35
  38.9 1.7 %collective-permute-done.1 = f32[136,128]{1,0:T(8,128)S(1)} collective-permute-done((f32[136,128]{1,0:T(8,128)S(1)}, f32[136,128]{1,0:T(8,128)S(1)}, u32[]{:S(2)}, u32[]{:S(2)}) %collective-permute-start.1) | collective-permute-done | bytes 69664 | tf_op jit(solution)/shard_map/ppermute | solution.py:35
  40.6 6.9 %collective-permute-start.2 = (f32[136,128]{1,0:T(8,128)S(1)}, f32[136,128]{1,0:T(8,128)S(1)}, u32[]{:S(2)}, u32[]{:S(2)}) collective-permute-start(f32[136,128]{1,0:T(8,128)S(1)} %add.25), channel_id=1, source_target_pairs={{0,128},{32,160},{64,192},{96,224},{128,0},{160,32},{192,64},{224,... | collective-permute-start | bytes 208904 | tf_op jit(solution)/shard_map/ppermute | solution.py:35
  47.5 2.4 %collective-permute-done.2 = f32[136,128]{1,0:T(8,128)S(1)} collective-permute-done((f32[136,128]{1,0:T(8,128)S(1)}, f32[136,128]{1,0:T(8,128)S(1)}, u32[]{:S(2)}, u32[]{:S(2)}) %collective-permute-start.2) | collective-permute-done | bytes 69664 | tf_op jit(solution)/shard_map/ppermute | solution.py:35
  50.1 15.5 %all_to_all.21 = f32[16,136,128]{2,1,0:T(8,128)S(1)} all-to-all(f32[16,136,128]{2,1,0:T(8,128)S(1)} %broadcast_in_dim.4), channel_id=1, replica_groups=mesh['uz'=8,'uy'=4,'ux'=4,'samp'=2] {'uy','ux'}, dimensions={0} | all-to-all | bytes 2228224 | tf_op jit(solution)/shard_map/all_to_all | solution.py:27
  68.5 8.1 %fusion.18 = f32[128,1024]{1,0:T(8,128)S(1)} fusion(f32[16,128,128]{1,2,0:T(8,128)S(1)} %fusion.26, f32[1024,2048]{1,0:T(8,128)} %param.3), kind=kOutput, calls=%fused_computation.14 | convolution fusion | flops 1610612736 | bytes 9961472 | tf_op jit(solution)/shard_map/jks,ujs->ku/dot_general | solution.py:57
  76.7 6.5 %collective-permute-start.3 = (f32[128,1152]{1,0:T(8,128)S(1)}, f32[128,1152]{1,0:T(8,128)S(1)}, u32[]{:S(2)}, u32[]{:S(2)}) collective-permute-start(f32[128,1152]{1,0:T(8,128)S(1)} %pad_maximum_fusion.2), channel_id=1, source_target_pairs={{0,1},{1,0},{2,3},{3,2},{4,5},{5,4},{6,7},{7,6},{8,9},{9,8},{10,11... | collective-permute-start | bytes 1769480 | tf_op jit(solution)/shard_map/ppermute | solution.py:53
  83.2 1.6 %collective-permute-done.3 = f32[128,1152]{1,0:T(8,128)S(1)} collective-permute-done((f32[128,1152]{1,0:T(8,128)S(1)}, f32[128,1152]{1,0:T(8,128)S(1)}, u32[]{:S(2)}, u32[]{:S(2)}) %collective-permute-start.3) | collective-permute-done | bytes 589856 | tf_op jit(solution)/shard_map/ppermute | solution.py:53
  85.8 3.3 %fusion.15 = f32[16,128,128]{2,1,0:T(8,128)S(1)} fusion(f32[128,1024]{1,0:T(8,128)S(1)} %fusion.29, f32[1024,2048]{1,0:T(8,128)S(1)} %bitcast.108), kind=kOutput, calls=%fused_computation.13 | convolution fusion | flops 1610612736 | bytes 9961472 | tf_op jit(solution)/shard_map/ku,ujs->jks/dot_general | solution.py:57
  89.2 20.9 %all_to_all.22 = f32[16,136,128]{2,1,0:T(8,128)} all-to-all(f32[16,136,128]{2,1,0:T(8,128)S(1)} %pad_maximum_fusion.1), channel_id=1, replica_groups=mesh['uz'=8,'uy'=4,'ux'=4,'samp'=2] {'uy','ux'}, dimensions={0} | all-to-all | bytes 2228224 | tf_op jit(solution)/shard_map/all_to_all | solution.py:22
  110.1 1.3 reduce_sum.19
  111.6 3.1 %collective-permute-done.4 = f32[136,128]{1,0:T(8,128)S(1)} collective-permute-done((f32[136,128]{1,0:T(8,128)S(1)}, f32[136,128]{1,0:T(8,128)S(1)}, u32[]{:S(2)}, u32[]{:S(2)}) %collective-permute-start.4) | collective-permute-done | bytes 69664 | tf_op jit(solution)/shard_map/ppermute | solution.py:35
  115.7 3.7 %collective-permute-done.5 = f32[136,128]{1,0:T(8,128)S(1)} collective-permute-done((f32[136,128]{1,0:T(8,128)S(1)}, f32[136,128]{1,0:T(8,128)S(1)}, u32[]{:S(2)}, u32[]{:S(2)}) %collective-permute-start.5) | collective-permute-done | bytes 69664 | tf_op jit(solution)/shard_map/ppermute | solution.py:35
  119.3 5.5 %collective-permute-start.6 = (f32[136,128]{1,0:T(8,128)S(1)}, f32[136,128]{1,0:T(8,128)S(1)}, u32[]{:S(2)}, u32[]{:S(2)}) collective-permute-start(f32[136,128]{1,0:T(8,128)S(1)} %add.29), channel_id=1, source_target_pairs={{0,128},{32,160},{64,192},{96,224},{128,0},{160,32},{192,64},{224,... | collective-permute-start | bytes 208904 | tf_op jit(solution)/shard_map/ppermute | solution.py:35
  124.9 1.8 %collective-permute-done.6 = f32[136,128]{1,0:T(8,128)S(1)} collective-permute-done((f32[136,128]{1,0:T(8,128)S(1)}, f32[136,128]{1,0:T(8,128)S(1)}, u32[]{:S(2)}, u32[]{:S(2)}) %collective-permute-start.6) | collective-permute-done | bytes 69664 | tf_op jit(solution)/shard_map/ppermute | solution.py:35
  126.9 16.1 %all_to_all.23 = f32[16,136,128]{2,1,0:T(8,128)S(1)} all-to-all(f32[16,136,128]{2,1,0:T(8,128)S(1)} %broadcast_in_dim.5), channel_id=1, replica_groups=mesh['uz'=8,'uy'=4,'ux'=4,'samp'=2] {'uy','ux'}, dimensions={0} | all-to-all | bytes 2228224 | tf_op jit(solution)/shard_map/all_to_all | solution.py:27
  144.7 8.0 %fusion.21 = f32[128,1024]{1,0:T(8,128)S(1)} fusion(f32[16,128,128]{1,2,0:T(8,128)S(1)} %get-tuple-element.4, f32[1024,2048]{1,0:T(8,128)} %param.3), kind=kOutput, calls=%fused_computation.15 | convolution fusion | flops 1610612736 | bytes 9961472 | tf_op jit(solution)/shard_map/jks,ujs->ku/dot_general | solution.py:57
  152.7 5.7 %collective-permute-start.7 = (f32[128,1152]{1,0:T(8,128)S(1)}, f32[128,1152]{1,0:T(8,128)S(1)}, u32[]{:S(2)}, u32[]{:S(2)}) collective-permute-start(f32[128,1152]{1,0:T(8,128)S(1)} %pad_maximum_fusion.3), channel_id=1, source_target_pairs={{0,1},{1,0},{2,3},{3,2},{4,5},{5,4},{6,7},{7,6},{8,9},{9,8},{10,11... | collective-permute-start | bytes 1769480 | tf_op jit(solution)/shard_map/ppermute | solution.py:53
  158.4 1.4 multiply_divide_fusion
  (55 shorter events, 9.2 us)
Async XLA Ops:
  1.9 33.9 %copy-start.3 = (f32[1024,128]{0,1:T(8,128)}, f32[1024,128]{0,1:T(8,128)S(1)}, u32[]{:S(2)}) copy-start(f32[1024,128]{0,1:T(8,128)S(1)} %copy.5) | copy-start | bytes 1572868
  2.3 63.4 %copy-start = (f32[2048,128]{1,0:T(8,128)S(1)}, f32[2048,128]{1,0:T(8,128)}, u32[]{:S(2)}) copy-start(f32[2048,128]{1,0:T(8,128)} %param.5) | copy-start | bytes 3145732
  32.4 3.4 %collective-permute-start = (f32[136,128]{1,0:T(8,128)S(1)}, f32[136,128]{1,0:T(8,128)S(1)}, u32[]{:S(2)}, u32[]{:S(2)}) collective-permute-start(f32[136,128]{1,0:T(8,128)S(1)} %reduce_sum.18), channel_id=1, source_target_pairs={{0,32},{32,0},{64,96},{96,64},{128,160},{160,128},{192,224},{224,1... | collective-permute-start | bytes 208904 | tf_op jit(solution)/shard_map/ppermute | solution.py:35
  35.8 4.8 %collective-permute-start.1 = (f32[136,128]{1,0:T(8,128)S(1)}, f32[136,128]{1,0:T(8,128)S(1)}, u32[]{:S(2)}, u32[]{:S(2)}) collective-permute-start(f32[136,128]{1,0:T(8,128)S(1)} %add.24), channel_id=1, source_target_pairs={{0,64},{32,96},{64,0},{96,32},{128,192},{160,224},{192,128},{224,1... | collective-permute-start | bytes 208904 | tf_op jit(solution)/shard_map/ppermute | solution.py:35
  40.6 9.3 %collective-permute-start.2 = (f32[136,128]{1,0:T(8,128)S(1)}, f32[136,128]{1,0:T(8,128)S(1)}, u32[]{:S(2)}, u32[]{:S(2)}) collective-permute-start(f32[136,128]{1,0:T(8,128)S(1)} %add.25), channel_id=1, source_target_pairs={{0,128},{32,160},{64,192},{96,224},{128,0},{160,32},{192,64},{224,... | collective-permute-start | bytes 208904 | tf_op jit(solution)/shard_map/ppermute | solution.py:35
  66.3 1.0 copy-start.1
  67.5 17.4 %copy-start.4 = (f32[1024,128]{0,1:T(8,128)S(1)}, f32[1024,128]{0,1:T(8,128)}, u32[]{:S(2)}) copy-start(f32[1024,128]{0,1:T(8,128)} %copy-done.3) | copy-start | bytes 1572868
  67.5 18.3 %slice-start = ((s8[8388608]{0:T(1024)(128)(4,1)}), s8[4194304]{0:T(1024)(128)(4,1)S(1)}, s32[]{:S(2)}) async-start(s8[8388608]{0:T(1024)(128)(4,1)} %bitcast.107), calls=%async_computation.4 | async-start | bytes 8388608
  68.5 17.3 %slice-start.1 = ((s8[8388608]{0:T(1024)(128)(4,1)}), s8[4194304]{0:T(1024)(128)(4,1)S(1)}, s32[]{:S(2)}) async-start(s8[8388608]{0:T(1024)(128)(4,1)} %bitcast.107), calls=%async_computation.5 | async-start | bytes 8388608
  76.7 8.1 %collective-permute-start.3 = (f32[128,1152]{1,0:T(8,128)S(1)}, f32[128,1152]{1,0:T(8,128)S(1)}, u32[]{:S(2)}, u32[]{:S(2)}) collective-permute-start(f32[128,1152]{1,0:T(8,128)S(1)} %pad_maximum_fusion.2), channel_id=1, source_target_pairs={{0,1},{1,0},{2,3},{3,2},{4,5},{5,4},{6,7},{7,6},{8,9},{9,8},{10,11... | collective-permute-start | bytes 1769480 | tf_op jit(solution)/shard_map/ppermute | solution.py:53
  85.4 3.7 %copy-start.5 = (f32[128,1024]{1,0:T(8,128)}, f32[128,1024]{1,0:T(8,128)S(1)}, u32[]{:S(2)}) copy-start(f32[128,1024]{1,0:T(8,128)S(1)} %fusion.29) | copy-start | bytes 1572868
  111.5 3.2 %collective-permute-start.4 = (f32[136,128]{1,0:T(8,128)S(1)}, f32[136,128]{1,0:T(8,128)S(1)}, u32[]{:S(2)}, u32[]{:S(2)}) collective-permute-start(f32[136,128]{1,0:T(8,128)S(1)} %reduce_sum.19), channel_id=1, source_target_pairs={{0,32},{32,0},{64,96},{96,64},{128,160},{160,128},{192,224},{224,1... | collective-permute-start | bytes 208904 | tf_op jit(solution)/shard_map/ppermute | solution.py:35
  114.7 4.6 %collective-permute-start.5 = (f32[136,128]{1,0:T(8,128)S(1)}, f32[136,128]{1,0:T(8,128)S(1)}, u32[]{:S(2)}, u32[]{:S(2)}) collective-permute-start(f32[136,128]{1,0:T(8,128)S(1)} %add.28), channel_id=1, source_target_pairs={{0,64},{32,96},{64,0},{96,32},{128,192},{160,224},{192,128},{224,1... | collective-permute-start | bytes 208904 | tf_op jit(solution)/shard_map/ppermute | solution.py:35
  119.3 7.3 %collective-permute-start.6 = (f32[136,128]{1,0:T(8,128)S(1)}, f32[136,128]{1,0:T(8,128)S(1)}, u32[]{:S(2)}, u32[]{:S(2)}) collective-permute-start(f32[136,128]{1,0:T(8,128)S(1)} %add.29), channel_id=1, source_target_pairs={{0,128},{32,160},{64,192},{96,224},{128,0},{160,32},{192,64},{224,... | collective-permute-start | bytes 208904 | tf_op jit(solution)/shard_map/ppermute | solution.py:35
  143.0 15.4 %copy-start.2 = (f32[128,2048]{0,1:S(1)}, f32[128,2048]{0,1}, u32[]{:S(2)}) copy-start(f32[128,2048]{0,1} %copy-done.1) | copy-start | bytes 3145732
  144.6 15.5 %copy-start.6 = (f32[128,1024]{1,0:T(8,128)S(1)}, f32[128,1024]{1,0:T(8,128)}, u32[]{:S(2)}) copy-start(f32[128,1024]{1,0:T(8,128)} %copy-done.5) | copy-start | bytes 1572868
  152.7 7.4 %collective-permute-start.7 = (f32[128,1152]{1,0:T(8,128)S(1)}, f32[128,1152]{1,0:T(8,128)S(1)}, u32[]{:S(2)}, u32[]{:S(2)}) collective-permute-start(f32[128,1152]{1,0:T(8,128)S(1)} %pad_maximum_fusion.3), channel_id=1, source_target_pairs={{0,1},{1,0},{2,3},{3,2},{4,5},{5,4},{6,7},{7,6},{8,9},{9,8},{10,11... | collective-permute-start | bytes 1769480 | tf_op jit(solution)/shard_map/ppermute | solution.py:53
